TPU v7x, 128 devices: a whole 4x4x4 slice. The times are simulated.
128 devices in a mesh: row: 4 (over x_lo, core), col: 32 (over y, x_hi, z).
Axes of the slice: x: 4 (x_hi: 2, x_lo: 2; x = x_hi * 2 + x_lo), y: 4, z: 4, core: 2. Of those that a mesh axis runs over, the one named last changes fastest.
Arguments:
- tokens: bfloat16 [8192, 2048], P('col', 'row'), may hold values from -40 to 40
- router: bfloat16 [2048, 64], replicated, may hold values from -0.375 to 0.375
- expert_ids: int32 [8192, 6], P('col'), may hold values from 0 to 63, all different within a row; in each aligned block of 256 rows (0 to 255, 256 to 511, ...) at most 32 rows name the same one
- expert_in: bfloat16 [64, 2, 2048, 1408], P('col', None, None, 'row'), may hold values from -0.125 to 0.125
- expert_out: bfloat16 [64, 1408, 2048], P('col', 'row'), may hold values from -0.15625 to 0.15625
- shared_in: bfloat16 [2, 2048, 2816], P(None, 'col', 'row'), may hold values from -0.125 to 0.125
- shared_out: bfloat16 [2816, 2048], P('row', 'col'), may hold values from -0.109375 to 0.109375
- kv_cache: bfloat16 [2, 2, 2, 32, 512, 2048], P(None, None, None, 'col', None, 'row'), may hold values from -6 to 6
- lengths: int32 [2], replicated, may hold values from 128 to 16384, as said below
- kv_proj: bfloat16 [2048, 2, 2048], P(None, None, 'row'), may hold values from -0.125 to 0.125
Outputs:
- mixed_out: bfloat16 [8192, 2048], P('col', 'row')
- cache_out: bfloat16 [2, 2, 2, 32, 512, 2048], P(None, None, None, None, ('row', 'col'))
Inputs may be any that keep to these rules, and one draw needn't show every extreme that they name: `expert_ids`: each token names 6 different experts; among the 256 tokens of one aligned block no expert is named by more than 32 tokens, and in some blocks one is named by exactly 32. `lengths`: exactly 1 entries are 16384; each other entry is at least 128 and at most 256.
All inputs are finite; a program needn't handle non-finite values.
Results may differ from a plain program's by a relative error of at most 0.013.
Values may be sent and summed in bfloat16 or wider, within the bound.
No kernel may reach another device: no remote copies, remote signals or barrier semaphores. Data moves between devices by JAX's collectives and lax.ppermute only.
A program may use at most 128 MiB of HBM per device.

v0:
```python
import jax
import jax.numpy as jnp
from jax import lax
from jax.sharding import PartitionSpec as P

CTX = 16384
CAP = 32


def relay_slabs(chosen, row_count, col_count):
    layers = chosen.shape[0]
    pairs = chosen.shape[1]
    requests = chosen.shape[2]
    slab_len = chosen.shape[4]
    head_width = chosen.shape[5]
    groups = layers * pairs * requests
    sectioned = chosen.reshape(groups, 1, slab_len, head_width)
    piece_len = slab_len // (row_count * col_count)
    relaid = lax.all_to_all(sectioned, ("row", "col"), split_axis=2, concat_axis=1, tiled=True)
    relaid = relaid.reshape(groups, row_count, col_count, piece_len, head_width)
    relaid = relaid.transpose(0, 2, 3, 1, 4).reshape(
        groups, col_count, piece_len, row_count * head_width
    )
    return relaid.reshape(layers, pairs, requests, col_count, piece_len, row_count * head_width)


def local(
    tokens,
    router,
    expert_ids,
    expert_in,
    expert_out,
    shared_in,
    shared_out,
    kv_cache,
    lengths,
    kv_proj,
):
    row_count = lax.axis_size("row")
    col_count = lax.axis_size("col")
    row_index = lax.axis_index("row")
    col_index = lax.axis_index("col")
    tok_rows = tokens.shape[0]
    slice_width = tokens.shape[1]
    gathered = lax.all_gather(tokens, "row", axis=1, tiled=True)
    tokens_f = gathered.astype(jnp.float32)
    normed = (
        tokens_f * lax.rsqrt(jnp.mean(tokens_f * tokens_f, axis=-1, keepdims=True) + 1e-06)
    ).astype(jnp.bfloat16)
    logits = jnp.dot(normed, router, preferred_element_type=jnp.float32)
    expert_total = router.shape[1]
    top_count = expert_ids.shape[1]
    catalog = jnp.arange(expert_total, dtype=jnp.int32)
    matches = expert_ids[:, :, None] == catalog
    picked = jnp.sum(jnp.where(matches, logits[:, None, :], 0.0), axis=2)
    sigmoids = jax.nn.sigmoid(picked)
    gate_weights = sigmoids / jnp.sum(sigmoids, axis=1, keepdims=True)
    flat_ids = expert_ids.reshape(-1)
    onehot = (flat_ids[:, None] == catalog).astype(jnp.int32)
    slot_index = jnp.sum(onehot * (jnp.cumsum(onehot, axis=0) - 1), axis=1)
    dest_index = flat_ids * CAP + slot_index
    pair_token = jnp.arange(tok_rows * top_count, dtype=jnp.int32) // top_count
    source = jnp.full((expert_total * CAP,), -1, jnp.int32).at[dest_index].set(pair_token)
    filled = (source >= 0)[:, None]
    safe_source = jnp.maximum(source, 0)
    local_experts = expert_total // col_count
    empty_value = jnp.zeros((), jnp.bfloat16)
    outgoing = jnp.where(filled, normed[safe_source], empty_value).reshape(
        col_count, local_experts, CAP, -1
    )
    incoming = lax.all_to_all(outgoing, "col", split_axis=0, concat_axis=0, tiled=True)
    gate_up = jnp.einsum(
        "secd,egdf->gsecf", incoming, expert_in, preferred_element_type=jnp.float32
    )
    hidden = (jax.nn.silu(gate_up[0]) * gate_up[1]).astype(jnp.bfloat16)
    partial_out = jnp.einsum(
        "secf,efd->secd", hidden, expert_out, preferred_element_type=jnp.float32
    )
    summed = lax.psum_scatter(
        partial_out.astype(jnp.bfloat16), "row", scatter_dimension=3, tiled=True
    )
    returned = lax.all_to_all(summed, "col", split_axis=0, concat_axis=0, tiled=True).reshape(
        expert_total * CAP, slice_width
    )
    routed = returned[dest_index].reshape(tok_rows, top_count, slice_width).astype(jnp.float32)
    routed_sum = jnp.sum(gate_weights[:, :, None] * routed, axis=1)
    shared_acc = jnp.einsum(
        "td,gdf->gtf",
        normed,
        lax.all_gather(shared_in, "col", axis=1, tiled=True),
        preferred_element_type=jnp.float32,
    )
    shared_hidden = (jax.nn.silu(shared_acc[0]) * shared_acc[1]).astype(jnp.bfloat16)
    shared_terms = jnp.dot(
        shared_hidden,
        lax.all_gather(shared_out, "col", axis=1, tiled=True),
        preferred_element_type=jnp.float32,
    )
    shared_part = lax.psum_scatter(
        shared_terms.astype(jnp.bfloat16), "row", scatter_dimension=1, tiled=True
    ).astype(jnp.float32)
    mixed_out = (shared_part + routed_sum).astype(jnp.bfloat16)
    layers = kv_cache.shape[0]
    pairs = kv_cache.shape[1]
    requests = kv_cache.shape[2]
    slab_len = kv_cache.shape[4]
    head_slice = kv_cache.shape[5]
    piece_len = slab_len // (row_count * col_count)
    device_total = row_count * col_count
    span_local = jnp.einsum(
        "td,dph->tph", normed, kv_proj, preferred_element_type=jnp.float32
    ).astype(jnp.bfloat16)
    first_pos = CTX - tok_rows * col_count
    send_index = (
        first_pos + col_index * tok_rows + jnp.arange(tok_rows, dtype=jnp.int32)
    ) % slab_len
    outbound = jnp.zeros((slab_len, pairs, head_slice), jnp.bfloat16).at[send_index].set(span_local)
    outbound = outbound.reshape(device_total, piece_len, pairs, head_slice)
    inbound = lax.all_to_all(outbound, ("row", "col"), split_axis=0, concat_axis=0, tiled=True)
    inbound = inbound.reshape(row_count, col_count, piece_len, pairs, head_slice)
    device_flat = row_index * col_count + col_index
    source_block = jnp.arange(col_count, dtype=jnp.int32)[:, None]
    within = device_flat * piece_len + jnp.arange(piece_len, dtype=jnp.int32)[None, :]
    offset_tok = (within - first_pos - source_block * tok_rows) % slab_len
    usable = offset_tok < tok_rows
    slab_of = (first_pos + source_block * tok_rows + offset_tok) // slab_len
    slab_ids = jnp.arange(col_count, dtype=jnp.int32)[:, None, None]
    placing = ((slab_of[None, :, :] == slab_ids) & usable[None, :, :]).astype(jnp.bfloat16)
    placed = jnp.einsum("sck,rckph->pskrh", placing, inbound, preferred_element_type=jnp.float32)
    placed = placed.reshape(pairs, col_count, piece_len, row_count * head_slice).astype(
        jnp.bfloat16
    )
    covered = jnp.sum(placing.astype(jnp.float32), axis=1) > 0.5
    first_long = jnp.min(jnp.where(lengths == CTX, jnp.arange(requests, dtype=jnp.int32), requests))
    relaid = relay_slabs(kv_cache, row_count, col_count)
    start_pos = (row_index * col_count + col_index) * piece_len
    places = (
        jnp.arange(col_count, dtype=jnp.int32)[:, None] * slab_len
        + start_pos
        + jnp.arange(piece_len, dtype=jnp.int32)[None, :]
    )
    live_mask = places[None, :, :] < lengths[:, None, None]
    cache_out = jnp.where(live_mask[None, None, :, :, :, None], relaid, jnp.zeros((), relaid.dtype))
    layer_pick = (jnp.arange(layers, dtype=jnp.int32) == layers - 1)[
        :, None, None, None, None, None
    ]
    request_pick = (jnp.arange(requests, dtype=jnp.int32) == first_long)[
        None, None, :, None, None, None
    ]
    select = layer_pick & request_pick & covered[None, None, None, :, :, None]
    cache_out = jnp.where(select, placed[None, :, None], cache_out)
    return (mixed_out, cache_out)


def solution(mesh):
    return jax.shard_map(
        local,
        mesh=mesh,
        in_specs=(
            P("col", "row"),
            P(),
            P("col", None),
            P("col", None, None, "row"),
            P("col", "row", None),
            P(None, "col", "row"),
            P("row", "col"),
            P(None, None, None, "col", None, "row"),
            P(),
            P(None, None, "row"),
        ),
        out_specs=(P("col", "row"), P(None, None, None, None, ("row", "col"), None)),
        check_vma=False,
    )
```

profile of v0, /device:TPU:1, one launch (start us, length us, event | category | flops | bytes accessed | tf_op | source)
XLA Modules:
  0.0 478.3 jit_solution(9358178173785698817)
XLA Ops:
  7.2 0.7 all-gather.4.cloned.1.call-update
  8.0 0.7 all-gather.6.cloned.1.call-update
  8.7 0.7 broadcast_multiply_fusion
  9.4 0.8 copy.73
  10.8 0.8 fusion.26
  11.7 31.5 %reduce-window.6 = s32[64,12,128]{2,1,0:T(8,128)S(1)} reduce-window(s32[64,12,128]{2,1,0:T(8,128)} %fusion.26, s32[]{:T(128)} %constant.51.clone.1), window={size=1x1x128 pad=0_0x0_0x127_0}, to_apply=%region_4.5 | reduce-window | flops 12484608 | bytes 786436 | tf_op jit(solution)/shard_map/reduce-window
  43.2 1.0 slice.30
  44.2 1.3 copy.75
  46.0 6.2 %scatter_custom_fusion = s32[2048]{0:T(1024)S(1)} fusion(s32[1536]{0:T(1024)S(1)} %fusion.40, s32[1536]{0:T(1024)S(1)} %add_select_fusion, s32[]{:T(128)} %constant.46.clone.1), kind=kCustom, calls=%fused_computation.73 | custom fusion | bytes 8196 | tf_op jit(solution)/shard_map/scatter | solution.py:63
  52.3 1.5 fusion.13
  53.8 2.4 fusion.14
  56.3 17.7 %gather_fusion = bf16[2048,2048]{1,0:T(8,128)(2,1)} fusion(bf16[256,2048]{1,0:T(8,128)(2,1)} %fusion.14, s32[2048]{0:T(1024)S(1)} %maximum_clamp_fusion), kind=kCustom, calls=%fused_computation | custom fusion | bytes 16785408 | tf_op jit(solution)/shard_map/gather | solution.py:68
  74.0 7.4 %broadcast_select_fusion = bf16[32,2,32,2048]{3,2,1,0:T(8,128)(2,1)} fusion(bf16[32,2,32,2048]{3,2,1,0:T(8,128)(2,1)} %bitcast.92, pred[32,2,32]{2,1,0:T(4,128)(4,1)S(1)} %broadcast_in_dim.95), kind=kLoop, calls=%fused_computation.7 | loop fusion | flops 4194304 | bytes 16779264 | tf_op jit(solution)/shard_map/jit(_where)/select_n | solution.py:68
  81.3 129.2 %all_to_all.24 = bf16[32,2,32,2048]{3,2,1,0:T(8,128)(2,1)S(1)} all-to-all(bf16[32,2,32,2048]{3,2,1,0:T(8,128)(2,1)} %broadcast_select_fusion), channel_id=1, replica_groups=mesh['row'=4,'col'=32] {'col'}, dimensions={0} | all-to-all | bytes 16777216 | tf_op jit(solution)/shard_map/all_to_all | solution.py:71
  210.6 8.7 %fusion.8 = f32[2,32,2,32,352]{4,3,0,1,2:T(8,128)S(1)} fusion(bf16[2,2,2048,352]{2,3,1,0:T(8,128)(2,1)} %param.13, bf16[32,2,32,2048]{3,2,1,0:T(8,128)(2,1)S(1)} %all_to_all.24), kind=kOutput, calls=%fused_computation.18 | convolution fusion | flops 5905580032 | bytes 19922944 | tf_op jit(solution)/shard_map/secd,egdf->gsecf/dot_general | solution.py:72
  219.3 6.8 %convert_bitcast_fusion = bf16[32,2,32,2048]{3,2,0,1:T(8,128)(2,1)} fusion(bf16[2,352,2048]{2,1,0:T(8,128)(2,1)S(1)} %copy-done, f32[2,32,2,32,352]{4,3,0,1,2:T(8,128)S(1)} %fusion.8), kind=kOutput, calls=%fused_computation.6 | convolution fusion | flops 2961309696 | bytes 17039360 | tf_op jit(solution)/shard_map/secf,efd->secd/dot_general | solution.py:76
  226.2 0.2 all-gather.8.cloned.1.call-start
  226.4 0.3 all-gather.8.cloned.1.call-update
  226.8 0.6 copy-done.2
  227.4 3.4 fusion.18
  230.8 0.5 copy.81
  231.3 1.5 broadcast_in_dim.101
  232.9 26.9 %scatter_fusion = bf16[512,2,512]{2,1,0:T(2,128)(2,1)} fusion(bf16[512,2,512]{2,1,0:T(2,128)(2,1)} %broadcast_in_dim.101, s32[256]{0:T(256)S(1)} %bitcast.98, bf16[256,2,512]{2,1,0:T(2,128)(2,1)S(1)} %copy.81), kind=kCustom, calls=%fused_computation.3 | custom fusion | bytes 1573888 | tf_op jit(solution)/shard_map/scatter | solution.py:117
  259.8 5.8 %all-to-all-start.2 = ((bf16[128,4,2,512]{3,2,1,0:T(2,128)(2,1)}), bf16[128,4,2,512]{3,2,1,0:T(2,128)(2,1)S(1)}, u32[]{:S(2)}, u32[]{:S(2)}) async-start(bf16[128,4,2,512]{3,2,1,0:T(2,128)(2,1)} %bitcast.18), calls=%async_computation.4 | async-start | bytes 2097152 | tf_op jit(solution)/shard_map/all_to_all | solution.py:119
  265.6 6.8 %copy.96 = bf16[8,1,512,512]{3,0,1,2:T(8,128)(2,1)} copy(bf16[8,1,512,512]{3,2,0,1:T(8,128)(2,1)} %bitcast.93) | data formatting | bytes 8388608 | tf_op jit(solution)/shard_map/reshape | solution.py:17
  272.4 23.4 %all-to-all-done.2 = bf16[128,4,2,512]{3,2,1,0:T(2,128)(2,1)S(1)} async-done(((bf16[128,4,2,512]{3,2,1,0:T(2,128)(2,1)}), bf16[128,4,2,512]{3,2,1,0:T(2,128)(2,1)S(1)}, u32[]{:S(2)}, u32[]{:S(2)}) %all-to-all-start.2) | async-done | bytes 1048608 | tf_op jit(solution)/shard_map/all_to_all | solution.py:119
  295.8 5.8 %all-to-all-start.3 = ((bf16[8,1,512,512]{3,0,1,2:T(8,128)(2,1)}), bf16[8,1,512,512]{3,0,1,2:T(8,128)(2,1)}, u32[]{:S(2)}, u32[]{:S(2)}) async-start(bf16[8,1,512,512]{3,0,1,2:T(8,128)(2,1)} %copy.96), calls=%async_computation.5 | async-start | bytes 8388608 | tf_op jit(solution)/shard_map/all_to_all | solution.py:19
  301.7 0.6 fusion.47
  302.4 0.6 iota_compare_fusion.4
  303.4 6.5 %convolution_bitcast_fusion = f32[2,256,704]{1,2,0:T(8,128)} fusion(bf16[2,2048,704]{2,1,0:T(8,128)(2,1)} %all-gather.6.cloned.1.call-done, bf16[256,2048]{1,0:T(8,128)(2,1)S(1)} %copy-done.2), kind=kOutput, calls=%fused_computation.26 | convolution fusion | flops 1476395008 | bytes 8257536 | tf_op jit(solution)/shard_map/td,gdf->gtf/dot_general | solution.py:87
  309.9 14.7 %reduce-scatter.5.cloned.1.call-done = bf16[32,2,32,512]{3,2,0,1:T(8,128)(2,1)} async-done(((bf16[32,2,32,2048]{3,2,0,1:T(8,128)(2,1)}), bf16[32,2,32,512]{3,2,0,1:T(8,128)(2,1)}) %reduce-scatter.5.cloned.1.call-update) | async-done | bytes 2097168 | tf_op jit(solution)/shard_map/reduce_scatter | solution.py:79
  324.6 3.2 copy.79
  327.8 35.9 %all-to-all-done.3 = bf16[8,1,512,512]{3,0,1,2:T(8,128)(2,1)} async-done(((bf16[8,1,512,512]{3,0,1,2:T(8,128)(2,1)}), bf16[8,1,512,512]{3,0,1,2:T(8,128)(2,1)}, u32[]{:S(2)}, u32[]{:S(2)}) %all-to-all-start.3) | async-done | bytes 4194336 | tf_op jit(solution)/shard_map/all_to_all | solution.py:19
  363.7 4.8 all-to-all-start.1
  368.5 55.5 %all-gather.8.cloned.1.call-done = bf16[704,2048]{0,1:T(8,128)(2,1)} async-done(((bf16[704,64]{0,1:T(8,128)(2,1)}), bf16[704,2048]{0,1:T(8,128)(2,1)}) %all-gather.8.cloned.1.call-update) | async-done | bytes 2883600 | tf_op jit(solution)/shard_map/all_gather | solution.py:96
  424.0 4.4 convolution_convert_fusion
  428.5 0.4 fusion.50
  429.2 0.6 fusion.17
  429.8 0.8 copy.84
  430.7 1.0 convert_element_type.77
  431.7 7.4 %copy.86 = bf16[8,32,4,4,512]{4,3,1,2,0:T(4,128)(2,1)} copy(bf16[8,32,4,4,512]{4,0,2,1,3:T(8,128)(2,1)} %bitcast.25) | data formatting | bytes 8388608 | tf_op jit(solution)/shard_map/transpose | solution.py:21
  439.1 7.8 %reshape_reshape.3 = bf16[2,2,2,32,4,2048]{5,3,4,2,1,0:T(8,128)(2,1)} reshape(bf16[8,32,4,4,512]{4,3,1,2,0:T(4,128)(2,1)} %copy.86) | data formatting | bytes 8388608 | tf_op jit(solution)/shard_map/reshape;reshape | solution.py:24
  447.0 2.7 select_select_fusion
  449.6 5.3 %copy.87 = bf16[2,2,2,32,4,2048]{5,4,3,2,1,0:T(4,128)(2,1)} copy(bf16[2,2,2,32,4,2048]{5,3,4,2,1,0:T(8,128)(2,1)S(1)} %select_select_fusion) | data formatting | bytes 8388608
  454.9 7.4 %gather_fusion.1 = bf16[1536,512]{1,0:T(8,128)(2,1)} fusion(bf16[2048,512]{1,0:T(8,128)(2,1)} %bitcast.16, s32[2048]{0:T(1024)S(1)} %pad_clamp_fusion), kind=kCustom, calls=%fused_computation.1 | custom fusion | bytes 3151872 | tf_op jit(solution)/shard_map/gather | solution.py:85
  462.3 4.2 reshape.362
  466.5 3.5 multiply_reduce_fusion
  470.0 1.7 add_convert_fusion
  (52 shorter events, 2.2 us)
Async XLA Ops:
  7.2 212.2 %copy-start = (bf16[2,352,2048]{2,1,0:T(8,128)(2,1)S(1)}, bf16[2,352,2048]{2,1,0:T(8,128)(2,1)}, u32[]{:S(2)}) copy-start(bf16[2,352,2048]{2,1,0:T(8,128)(2,1)} %param.14) | copy-start | bytes 8650756
  7.2 45.1 %all-gather.4.cloned.1.call-start = ((), (), s32[]{:S(2)}) async-start(), calls=%async_computation.6 | async-start | bytes 1310720 | tf_op jit(solution)/shard_map/all_gather | solution.py:45
  7.9 295.5 %all-gather.6.cloned.1.call-start = ((), (), s32[]{:S(2)}) async-start(), calls=%async_computation.7 | async-start | bytes 6488064 | tf_op jit(solution)/shard_map/all_gather | solution.py:90
  8.7 316.0 %reduce-scatter.5.cloned.1.call-start = ((), (), s32[]{:S(2)}) async-start(), calls=%async_computation.10 | async-start | bytes 10485760 | tf_op jit(solution)/shard_map/reduce_scatter | solution.py:79
  226.1 1.2 copy-start.2
  226.2 197.9 %all-gather.8.cloned.1.call-start = ((), (), s32[]{:S(2)}) async-start(), calls=%async_computation.8 | async-start | bytes 3244032 | tf_op jit(solution)/shard_map/all_gather | solution.py:96
  259.8 36.0 %all-to-all-start.2 = ((bf16[128,4,2,512]{3,2,1,0:T(2,128)(2,1)}), bf16[128,4,2,512]{3,2,1,0:T(2,128)(2,1)S(1)}, u32[]{:S(2)}, u32[]{:S(2)}) async-start(bf16[128,4,2,512]{3,2,1,0:T(2,128)(2,1)} %bitcast.18), calls=%async_computation.4 | async-start | bytes 2097152 | tf_op jit(solution)/shard_map/all_to_all | solution.py:119
  272.4 29.3 %copy-start.5 = (s32[2]{0:T(128)S(1)}, s32[2]{0:T(128)}, u32[]{:S(2)}) copy-start(s32[2]{0:T(128)} %param.18) | copy-start | bytes 28
  295.8 67.8 %all-to-all-start.3 = ((bf16[8,1,512,512]{3,0,1,2:T(8,128)(2,1)}), bf16[8,1,512,512]{3,0,1,2:T(8,128)(2,1)}, u32[]{:S(2)}, u32[]{:S(2)}) async-start(bf16[8,1,512,512]{3,0,1,2:T(8,128)(2,1)} %copy.96), calls=%async_computation.5 | async-start | bytes 8388608 | tf_op jit(solution)/shard_map/all_to_all | solution.py:19
  363.7 91.2 %all-to-all-start.1 = ((bf16[32,2,32,512]{3,2,1,0:T(8,128)(2,1)}), bf16[32,2,32,512]{3,2,1,0:T(8,128)(2,1)}, u32[]{:S(2)}, u32[]{:S(2)}) async-start(bf16[32,2,32,512]{3,2,1,0:T(8,128)(2,1)} %copy.79), calls=%async_computation.3 | async-start | bytes 4194304 | tf_op jit(solution)/shard_map/all_to_all | solution.py:82
  368.4 60.1 %copy-start.3 = (bf16[2048,64]{0,1:T(8,128)(2,1)S(1)}, bf16[2048,64]{0,1:T(8,128)(2,1)}, u32[]{:S(2)}) copy-start(bf16[2048,64]{0,1:T(8,128)(2,1)} %param.11) | copy-start | bytes 786436
  368.5 60.5 %copy-start.4 = (s32[256,6]{0,1:T(8,128)S(1)}, s32[256,6]{0,1:T(8,128)}, u32[]{:S(2)}) copy-start(s32[256,6]{0,1:T(8,128)} %param.12) | copy-start | bytes 18436
  368.5 101.6 %reduce-scatter.3.cloned.1.call-start = ((), (), s32[]{:S(2)}) async-start(), calls=%async_computation.9 | async-start | bytes 1310720 | tf_op jit(solution)/shard_map/reduce_scatter | solution.py:99
  462.3 9.5 %copy-start.1 = (bf16[2,352,2048]{2,1,0:T(8,128)(2,1)S(1)}, bf16[2,352,2048]{2,1,0:T(8,128)(2,1)}, u32[]{:S(2)}) copy-start(bf16[2,352,2048]{2,1,0:T(8,128)(2,1)} %param.14) | copy-start | bytes 8650756
Sparse Core Ops, SparseCore 0:
  9.7 24.3 all-gather.3
  37.1 154.4 all-gather.5
  226.3 98.2 reduce-scatter.4
  327.6 96.3 all-gather.7
  428.5 20.8 reduce-scatter.2
where the time goes:
time: 482 us; the launch traced here: 478 us
  waiting for transfers between devices  131 us (27%)
  blocking collectives  129 us (27%)
  local copies, waits for them, and re-layouts  101 us (21%)
  other arithmetic  54.6 us (11%)
  matrix products  30.8 us (6%)
  starting transfers between devices  16.8 us (3%)
  between operations  14.1 us (3%)
    all_to_all x1, blocking collectives, local(): lax.all_to_all(outgoing, 'col', split_axis=0, concat_axis=0, tiled=True)  129 us
    all_gather x1, waiting for transfers between devices, local(): lax.all_gather(shared_out, 'col', axis=1, tiled=True)  55.5 us
    all_to_all x1, waiting for transfers between devices, relay_slabs(): lax.all_to_all(sectioned, ('row', 'col'), split_axis=2, concat_axis=1, ti...  35.9 us
    another operation x2, other arithmetic  31.5 us
    scatter x1, local copies, waits for them, and re-layouts, local(): jnp.zeros((slab_len, pairs, head_slice), jnp.bfloat16).at[send_index]  26.9 us
    all_to_all x1, waiting for transfers between devices, local(): lax.all_to_all(outbound, ('row', 'col'), split_axis=0, concat_axis=0, til...  23.4 us
    gather x1, local copies, waits for them, and re-layouts, local(): normed[safe_source]  17.7 us
    reduce_scatter x1, waiting for transfers between devices, local(): lax.psum_scatter(partial_out.astype(jnp.bfloat16), 'row', scatter_dimensi...  14.7 us
  transfers between devices with their start and end apart: 8, of which 4 were waited for; matrix products, arithmetic and copies ran while one was open for 39% of the time, Pallas kernels for 0%

commit v1 on v0

v1 whole, which is shorter than its diff:
```python
import jax
import jax.numpy as jnp
from jax import lax
from jax.sharding import Mesh
from jax.sharding import PartitionSpec as P

CTX = 16384
CAP = 32
ROW = ("xl", "core")
COL = ("y", "xh", "z")
AXES = ROW + COL


def relay_slabs(chosen, row_count, col_count):
    layers = chosen.shape[0]
    pairs = chosen.shape[1]
    requests = chosen.shape[2]
    slab_len = chosen.shape[4]
    head_width = chosen.shape[5]
    groups = layers * pairs * requests
    sectioned = chosen.reshape(groups, 1, slab_len, head_width)
    piece_len = slab_len // (row_count * col_count)
    relaid = lax.all_to_all(sectioned, AXES, split_axis=2, concat_axis=1, tiled=True)
    relaid = relaid.reshape(groups, row_count, col_count, piece_len, head_width)
    relaid = relaid.transpose(0, 2, 3, 1, 4).reshape(
        groups, col_count, piece_len, row_count * head_width
    )
    return relaid.reshape(layers, pairs, requests, col_count, piece_len, row_count * head_width)


def row_order(x, dim):
    shape = x.shape
    quarter = shape[dim] // 4
    split = x.reshape(shape[:dim] + (2, 2, quarter) + shape[dim + 1 :])
    return jnp.swapaxes(split, dim, dim + 1).reshape(shape)


def row_reduce_scatter(x, dim):
    half = lax.psum_scatter(x, "core", scatter_dimension=dim, tiled=True)
    return lax.psum_scatter(half, "xl", scatter_dimension=dim, tiled=True)


def col_gather(x, dim):
    for name in ("z", "xh", "y"):
        x = lax.all_gather(x, name, axis=dim, tiled=True)
    return x


def local(
    tokens,
    router,
    expert_ids,
    expert_in,
    expert_out,
    shared_in,
    shared_out,
    kv_cache,
    lengths,
    kv_proj,
    row_count,
    col_count,
):
    row_index = lax.axis_index(ROW)
    col_index = lax.axis_index(COL)
    core_index = lax.axis_index("core")
    tok_rows = tokens.shape[0]
    slice_width = tokens.shape[1]
    gathered = lax.all_gather(tokens, "core", axis=1, tiled=True)
    gathered = lax.all_gather(gathered, "xl", axis=1, tiled=True)
    width = gathered.shape[1]
    half_width = width // 2
    tokens_f = gathered.astype(jnp.float32)
    normed = (
        tokens_f * lax.rsqrt(jnp.mean(tokens_f * tokens_f, axis=-1, keepdims=True) + 1e-06)
    ).astype(jnp.bfloat16)
    logits = jnp.dot(normed, router, preferred_element_type=jnp.float32)
    expert_total = router.shape[1]
    top_count = expert_ids.shape[1]
    catalog = jnp.arange(expert_total, dtype=jnp.int32)
    matches = expert_ids[:, :, None] == catalog
    picked = jnp.sum(jnp.where(matches, logits[:, None, :], 0.0), axis=2)
    sigmoids = jax.nn.sigmoid(picked)
    gate_weights = sigmoids / jnp.sum(sigmoids, axis=1, keepdims=True)
    flat_ids = expert_ids.reshape(-1)
    pair_count = flat_ids.shape[0]
    onehot = (flat_ids[:, None] == catalog).astype(jnp.bfloat16)
    pair_iota = jnp.arange(pair_count, dtype=jnp.int32)
    earlier = (pair_iota[None, :] < pair_iota[:, None]).astype(jnp.bfloat16)
    before = jnp.dot(earlier, onehot, preferred_element_type=jnp.float32)
    slot_index = jnp.sum(before * onehot.astype(jnp.float32), axis=1).astype(jnp.int32)
    dest_index = flat_ids * CAP + slot_index
    slot_total = expert_total * CAP
    slots = jnp.arange(slot_total, dtype=jnp.int32)
    dest_tok = dest_index.reshape(tok_rows, top_count)
    select_tok = jnp.any(dest_tok[None, :, :] == slots[:, None, None], axis=2).astype(jnp.bfloat16)
    local_experts = expert_total // col_count
    own_half = lax.dynamic_slice_in_dim(normed, core_index * half_width, half_width, axis=1)
    outgoing = jnp.dot(select_tok, own_half, preferred_element_type=jnp.float32)
    outgoing = outgoing.astype(jnp.bfloat16).reshape(col_count, local_experts, CAP, half_width)
    incoming_own = lax.all_to_all(outgoing, COL, split_axis=0, concat_axis=0, tiled=True)
    incoming_other = lax.ppermute(incoming_own, "core", perm=[(0, 1), (1, 0)])
    weights_own = lax.dynamic_slice_in_dim(expert_in, core_index * half_width, half_width, axis=2)
    weights_other = lax.dynamic_slice_in_dim(
        expert_in, (1 - core_index) * half_width, half_width, axis=2
    )
    gate_up = jnp.einsum(
        "secd,egdf->gsecf", incoming_own, weights_own, preferred_element_type=jnp.float32
    ) + jnp.einsum(
        "secd,egdf->gsecf", incoming_other, weights_other, preferred_element_type=jnp.float32
    )
    hidden = (jax.nn.silu(gate_up[0]) * gate_up[1]).astype(jnp.bfloat16)
    partial_out = jnp.einsum(
        "secf,efd->secd", hidden, row_order(expert_out, 2), preferred_element_type=jnp.float32
    )
    summed = row_reduce_scatter(partial_out.astype(jnp.bfloat16), 3)
    returned = lax.all_to_all(summed, COL, split_axis=0, concat_axis=0, tiled=True).reshape(
        slot_total, slice_width
    )
    pick = (dest_index[:, None] == slots[None, :]).astype(jnp.bfloat16)
    routed = jnp.dot(pick, returned, preferred_element_type=jnp.float32)
    routed = routed.reshape(tok_rows, top_count, slice_width)
    routed_sum = jnp.sum(gate_weights[:, :, None] * routed, axis=1)
    shared_acc = jnp.einsum(
        "td,gdf->gtf",
        normed,
        col_gather(shared_in, 1),
        preferred_element_type=jnp.float32,
    )
    shared_hidden = (jax.nn.silu(shared_acc[0]) * shared_acc[1]).astype(jnp.bfloat16)
    shared_terms = jnp.dot(
        shared_hidden,
        row_order(col_gather(shared_out, 1), 1),
        preferred_element_type=jnp.float32,
    )
    shared_part = row_reduce_scatter(shared_terms.astype(jnp.bfloat16), 1).astype(jnp.float32)
    mixed_out = (shared_part + routed_sum).astype(jnp.bfloat16)
    layers = kv_cache.shape[0]
    pairs = kv_cache.shape[1]
    requests = kv_cache.shape[2]
    slab_len = kv_cache.shape[4]
    head_slice = kv_cache.shape[5]
    piece_len = slab_len // (row_count * col_count)
    device_total = row_count * col_count
    span_local = jnp.einsum(
        "td,dph->tph", normed, kv_proj, preferred_element_type=jnp.float32
    ).astype(jnp.bfloat16)
    first_pos = CTX - tok_rows * col_count
    send_offset = (first_pos + col_index * tok_rows) % slab_len
    outbound = lax.dynamic_update_slice(
        jnp.zeros((slab_len, pairs, head_slice), jnp.bfloat16), span_local, (send_offset, 0, 0)
    )
    outbound = outbound.reshape(device_total, piece_len, pairs, head_slice)
    inbound = lax.all_to_all(outbound, AXES, split_axis=0, concat_axis=0, tiled=True)
    inbound = inbound.reshape(row_count, col_count, piece_len, pairs, head_slice)
    device_flat = row_index * col_count + col_index
    source_block = jnp.arange(col_count, dtype=jnp.int32)[:, None]
    within = device_flat * piece_len + jnp.arange(piece_len, dtype=jnp.int32)[None, :]
    offset_tok = (within - first_pos - source_block * tok_rows) % slab_len
    usable = offset_tok < tok_rows
    slab_of = (first_pos + source_block * tok_rows + offset_tok) // slab_len
    slab_ids = jnp.arange(col_count, dtype=jnp.int32)[:, None, None]
    placing = ((slab_of[None, :, :] == slab_ids) & usable[None, :, :]).astype(jnp.bfloat16)
    placed = jnp.einsum("sck,rckph->pskrh", placing, inbound, preferred_element_type=jnp.float32)
    placed = placed.reshape(pairs, col_count, piece_len, row_count * head_slice).astype(
        jnp.bfloat16
    )
    covered = jnp.sum(placing.astype(jnp.float32), axis=1) > 0.5
    first_long = jnp.min(jnp.where(lengths == CTX, jnp.arange(requests, dtype=jnp.int32), requests))
    relaid = relay_slabs(kv_cache, row_count, col_count)
    start_pos = (row_index * col_count + col_index) * piece_len
    places = (
        jnp.arange(col_count, dtype=jnp.int32)[:, None] * slab_len
        + start_pos
        + jnp.arange(piece_len, dtype=jnp.int32)[None, :]
    )
    live_mask = places[None, :, :] < lengths[:, None, None]
    cache_out = jnp.where(live_mask[None, None, :, :, :, None], relaid, jnp.zeros((), relaid.dtype))
    layer_pick = (jnp.arange(layers, dtype=jnp.int32) == layers - 1)[
        :, None, None, None, None, None
    ]
    request_pick = (jnp.arange(requests, dtype=jnp.int32) == first_long)[
        None, None, :, None, None, None
    ]
    select = layer_pick & request_pick & covered[None, None, None, :, :, None]
    cache_out = jnp.where(select, placed[None, :, None], cache_out)
    return (mixed_out, cache_out)


def solution(mesh):
    row_count = mesh.shape["row"]
    col_count = mesh.shape["col"]
    fine = Mesh(mesh.devices.reshape(2, row_count // 2, 4, 2, col_count // 8), AXES)

    def body(*args):
        return local(*args, row_count, col_count)

    return jax.shard_map(
        body,
        mesh=fine,
        in_specs=(
            P(COL, ROW),
            P(),
            P(COL, None),
            P(COL, None, None, ROW),
            P(COL, ROW, None),
            P(None, COL, ROW),
            P(ROW, COL),
            P(None, None, None, COL, None, ROW),
            P(),
            P(None, None, ROW),
        ),
        out_specs=(P(COL, ROW), P(None, None, None, None, AXES, None)),
        check_vma=False,
    )
```

time: 482 us -> 405 us (0.84)
  other arithmetic: 54.6 us -> 11.5 us
  blocking collectives: 129 us -> 94.2 us
  local copies, waits for them, and re-layouts: 101 us -> 70.1 us
  matrix products: 30.8 us -> 44.2 us
  starting transfers between devices: 16.8 us -> 28.7 us
    all_to_all x1, blocking collectives: 129 us -> 59.4 us  [local(): lax.all_to_all(outgoing, COL, split_axis=0, concat_axis=0, tiled=True)]
    all_gather x3 -> x4, waiting for transfers between devices: 55.5 us -> 103 us  [the longest x3 81.7 us: col_gather(): x = lax.all_gather(x, name, axis=dim, tiled=True)]
    all_gather x0 -> x4, blocking collectives: none -> 34.8 us  [the longest x3 29.6 us: col_gather(): x = lax.all_gather(x, name, axis=dim, tiled=True)]
    all_to_all x3, waiting for transfers between devices: 59.3 us -> 25.5 us  [the longest x1 23.6 us: local(): lax.all_to_all(outbound, AXES, split_axis=0, concat_axis=0, tiled=True)]
    scatter x2 -> x0, local copies, waits for them, and re-layouts: 33.1 us -> none  [the longest x1 26.9 us: local(): jnp.zeros((slab_len, pairs, head_slice), jnp.bfloat16).at[send_index]]
    another operation x2 -> x0, other arithmetic: 31.5 us -> none
    gather x2 -> x0, local copies, waits for them, and re-layouts: 25 us -> none  [the longest x1 17.7 us: local(): normed[safe_source]]
    reshape x0 -> x4, local copies, waits for them, and re-layouts: none -> 22.1 us  [the longest x2 15.4 us: row_order(): split = x.reshape(shape[:dim] + (2, 2, quarter) + shape[dim + 1:])]
  transfers between devices with their start and end apart: 8 -> 12, of which waited for: 4 -> 5; matrix products, arithmetic and copies ran while one was open for 39% -> 29% of each run, Pallas kernels for 0% -> 0%
where the time goes in v1:
time: 405 us; the launch traced here: 398 us
  waiting for transfers between devices  133 us (33%)
  blocking collectives  94.2 us (23%)
  local copies, waits for them, and re-layouts  70.1 us (17%)
  matrix products  44.2 us (11%)
  starting transfers between devices  28.7 us (7%)
  between operations  16.3 us (4%)
  other arithmetic  11.5 us (3%)
    all_gather x3, waiting for transfers between devices, col_gather(): x = lax.all_gather(x, name, axis=dim, tiled=True)  81.7 us
    all_to_all x1, blocking collectives, local(): lax.all_to_all(outgoing, COL, split_axis=0, concat_axis=0, tiled=True)  59.4 us
    all_gather x3, blocking collectives, col_gather(): x = lax.all_gather(x, name, axis=dim, tiled=True)  29.6 us
    all_to_all x1, waiting for transfers between devices, local(): lax.all_to_all(outbound, AXES, split_axis=0, concat_axis=0, tiled=True)  23.6 us
    all_gather x1, waiting for transfers between devices, local(): gathered = lax.all_gather(gathered, 'xl', axis=1, tiled=True)  21.2 us
    reshape x2, local copies, waits for them, and re-layouts, row_order(): split = x.reshape(shape[:dim] + (2, 2, quarter) + shape[dim + 1:])  15.4 us
    all_to_all x1, starting transfers between devices, local(): lax.all_to_all(outbound, AXES, split_axis=0, concat_axis=0, tiled=True)  11.9 us
    dot_general x1, matrix products, local(): jnp.einsum('secf,efd->secd', hidden, row_order(expert_out, 2), preferred_...  9.61 us
  transfers between devices with their start and end apart: 12, of which 5 were waited for; matrix products, arithmetic and copies ran while one was open for 29% of the time, Pallas kernels for 0%

profile of v1, /device:TPU:1, one launch (start us, length us, event | category | flops | bytes accessed | tf_op | source)
XLA Modules:
  0.0 397.8 jit_solution(841487472894106860)
XLA Ops:
  8.1 5.2 %all_gather.24 = bf16[256,1024]{1,0:T(8,128)(2,1)} all-gather(bf16[256,512]{1,0:T(8,128)(2,1)} %param.10), channel_id=1, replica_groups=mesh['xl'=2,'core'=2,'y'=4,'xh'=2,'z'=4] {'core'}, dimensions={1}, use_global_device_ids=true | all-gather | bytes 786432 | tf_op jit(solution)/shard_map/all_gather | solution.py:68
  13.4 0.8 copy.103
  14.3 1.0 fusion.34
  15.6 2.3 fusion.3
  17.9 21.2 %all-gather.5.cloned.1.call-done = bf16[256,2048]{1,0:T(8,128)(2,1)} async-done(((bf16[256,1024]{1,0:T(8,128)(2,1)}), bf16[256,2048]{1,0:T(8,128)(2,1)}) %all-gather.5.cloned.1.call-update) | async-done | bytes 1048592 | tf_op jit(solution)/shard_map/all_gather | solution.py:69
  39.1 1.5 fusion.24
  40.6 1.5 fusion.25
  42.1 1.3 convolution_convert_fusion
  43.3 59.4 %all_to_all.24 = bf16[32,2,32,1024]{3,2,1,0:T(8,128)(2,1)S(1)} all-to-all(bf16[32,2,32,1024]{3,2,1,0:T(8,128)(2,1)S(1)} %bitcast.89), channel_id=1, replica_groups=mesh['xl'=2,'core'=2,'y'=4,'xh'=2,'z'=4] {'y','xh','z'}, dimensions={0} | all-to-all | bytes 8388608 | tf_op jit(solution)/shard_map/all_to_all | solution.py:100
  102.8 2.8 copy.106
  105.5 2.0 collective-permute-start
  107.7 11.0 %all_gather.26 = bf16[2,256,704]{2,0,1:T(2,128)(2,1)S(1)} all-gather(bf16[2,64,704]{2,0,1:T(2,128)(2,1)S(1)} %copy.100), channel_id=1, replica_groups=mesh['xl'=2,'core'=2,'y'=4,'xh'=2,'z'=4] {'z'}, dimensions={1}, use_global_device_ids=true | all-gather | bytes 901120 | tf_op jit(solution)/shard_map/all_gather | solution.py:45
  118.8 1.9 copy.101
  121.0 7.7 %reshape.310 = bf16[2,352,2,2,512]{4,3,2,1,0:T(2,128)(2,1)} reshape(bf16[2,352,2048]{2,1,0:T(8,128)(2,1)} %param.14) | data formatting | bytes 5767168 | tf_op jit(solution)/shard_map/reshape | solution.py:34
  128.7 5.0 %copy.108 = bf16[2,352,2,2,512]{4,3,2,1,0:T(2,128)(2,1)S(1)} copy(bf16[2,352,2,2,512]{4,2,3,1,0:T(2,128)(2,1)} %bitcast.91) | data formatting | bytes 5767168 | tf_op jit(solution)/shard_map/transpose | solution.py:35
  133.7 3.3 reshape.322
  137.0 6.2 %fusion.8 = f32[2,2,352,32,32]{2,4,3,1,0:T(8,128)S(1)} fusion(bf16[2,2,2048,352]{2,3,1,0:T(8,128)(2,1)} %param.13, s32[]{:T(128)S(6)} %select_n.56, bf16[32,2,32,1024]{3,2,1,0:T(8,128)(2,1)} %copy-done.1), kind=kOutput, calls=%fused_computation.12 | convolution fusion | flops 2952790016 | bytes 12845060 | tf_op jit(solution)/shard_map/secd,egdf->gsecf/dot_general | solution.py:106
  143.3 9.4 %add_bitcast_fusion = f32[2,32,2,32,352]{4,3,1,0,2:T(8,128)} fusion(f32[2,2,352,32,32]{2,4,3,1,0:T(8,128)S(1)} %fusion.8, bf16[32,2,32,1024]{3,2,0,1:T(8,128)(2,1)} %collective-permute-done, bf16[2,2,2048,352]{2,3,1,0:T(8,128)(2,1)} %param.13, s32[]{:T(128)S(6)} %select_n.57), kind=kOutput, calls=%fused_computation.8 | convolution fusion | flops 2954231808 | bytes 18612228 | tf_op jit(solution)/shard_map/secd,egdf->gsecf/dot_general | solution.py:108
  152.6 9.6 %convert_bitcast_fusion = bf16[32,2,32,2048]{3,2,0,1:T(8,128)(2,1)} fusion(bf16[2,352,2048,1]{2,1,0,3:T(8,128)(2,1)S(1)} %copy-done.7, f32[2,32,2,32,352]{4,3,1,0,2:T(8,128)} %add_bitcast_fusion), kind=kOutput, calls=%fused_computation.7 | convolution fusion | flops 2961309696 | bytes 17039360 | tf_op jit(solution)/shard_map/secf,efd->secd/dot_general | solution.py:112
  162.3 0.8 copy-done.10
  163.1 9.6 %all_gather.29 = bf16[704,256]{0,1:T(8,128)(2,1)S(1)} all-gather(bf16[704,64]{0,1:T(8,128)(2,1)S(1)} %copy-done.10), channel_id=1, replica_groups=mesh['xl'=2,'core'=2,'y'=4,'xh'=2,'z'=4] {'z'}, dimensions={1}, use_global_device_ids=true | all-gather | bytes 450560 | tf_op jit(solution)/shard_map/all_gather | solution.py:45
  172.8 8.9 %all_gather.30 = bf16[704,512]{0,1:T(8,128)(2,1)} all-gather(bf16[704,256]{0,1:T(8,128)(2,1)S(1)} %all_gather.29), channel_id=1, replica_groups=mesh['xl'=2,'core'=2,'y'=4,'xh'=2,'z'=4] {'xh'}, dimensions={1}, use_global_device_ids=true | all-gather | bytes 1081344 | tf_op jit(solution)/shard_map/all_gather | solution.py:45
  183.0 3.4 fusion.31
  186.5 1.5 broadcast_in_dim.44
  188.0 1.3 copy_dynamic-update-slice_fusion
  189.3 11.9 %all-to-all-start.2 = ((bf16[128,4,2,512]{3,2,1,0:T(2,128)(2,1)}), bf16[128,4,2,512]{3,2,1,0:T(2,128)(2,1)S(1)}, u32[]{:S(2)}, u32[]{:S(2)}) async-start(bf16[128,4,2,512]{3,2,1,0:T(2,128)(2,1)} %bitcast.22), calls=%async_computation.6 | async-start | bytes 2097152 | tf_op jit(solution)/shard_map/all_to_all | solution.py:153
  201.2 6.6 %copy.128 = bf16[8,1,512,512]{3,0,1,2:T(8,128)(2,1)} copy(bf16[8,1,512,512]{3,2,0,1:T(8,128)(2,1)} %bitcast.92) | data formatting | bytes 8388608 | tf_op jit(solution)/shard_map/reshape | solution.py:21
  207.8 23.6 %all-to-all-done.2 = bf16[128,4,2,512]{3,2,1,0:T(2,128)(2,1)S(1)} async-done(((bf16[128,4,2,512]{3,2,1,0:T(2,128)(2,1)}), bf16[128,4,2,512]{3,2,1,0:T(2,128)(2,1)S(1)}, u32[]{:S(2)}, u32[]{:S(2)}) %all-to-all-start.2) | async-done | bytes 1048608 | tf_op jit(solution)/shard_map/all_to_all | solution.py:153
  231.5 1.0 copy-done.5
  232.4 5.8 %all-to-all-start.3 = ((bf16[8,1,512,512]{3,0,1,2:T(8,128)(2,1)}), bf16[8,1,512,512]{3,0,1,2:T(8,128)(2,1)}, u32[]{:S(2)}, u32[]{:S(2)}) async-start(bf16[8,1,512,512]{3,0,1,2:T(8,128)(2,1)} %copy.128), calls=%async_computation.7 | async-start | bytes 8388608 | tf_op jit(solution)/shard_map/all_to_all | solution.py:23
  239.0 0.6 iota_compare_fusion.12
  240.0 7.6 %copy.102 = bf16[704,2,2,512]{3,1,2,0:T(2,128)(2,1)S(1)} copy(bf16[704,2,2,512]{0,3,2,1:T(8,128)(2,1)} %bitcast.94) | data formatting | bytes 5767168 | tf_op jit(solution)/shard_map/reshape | solution.py:34
  247.6 3.4 reshape.308
  251.0 81.7 %all-gather.9.cloned.1.call-done = bf16[2,2048,704]{1,2,0:T(8,128)(2,1)} async-done(((bf16[2,512,704]{1,2,0:T(8,128)(2,1)}), bf16[2,2048,704]{1,2,0:T(8,128)(2,1)}) %all-gather.9.cloned.1.call-update) | async-done | bytes 5767184 | tf_op jit(solution)/shard_map/all_gather | solution.py:45
  332.6 4.7 %convolution_bitcast_fusion = f32[2,256,704]{1,2,0:T(8,128)S(1)} fusion(bf16[2,2048,704]{1,2,0:T(8,128)(2,1)} %all-gather.9.cloned.1.call-done, bf16[256,2048]{1,0:T(8,128)(2,1)} %copy-done.2), kind=kOutput, calls=%fused_computation.36 | convolution fusion | flops 1476395008 | bytes 8257536 | tf_op jit(solution)/shard_map/td,gdf->gtf/dot_general | solution.py:123
  337.4 2.1 convolution_convert_fusion.1
  339.6 3.3 copy.109
  343.0 8.3 %all-to-all-start.1 = ((bf16[32,2,32,512]{3,2,1,0:T(8,128)(2,1)}), bf16[32,2,32,512]{3,2,1,0:T(8,128)(2,1)}, u32[]{:S(2)}, u32[]{:S(2)}) async-start(bf16[32,2,32,512]{3,2,1,0:T(8,128)(2,1)} %copy.109), calls=%async_computation.5 | async-start | bytes 4194304 | tf_op jit(solution)/shard_map/all_to_all | solution.py:116
  352.6 0.8 copy.114
  353.4 1.1 convert_element_type.96
  354.5 7.4 %copy.116 = bf16[8,32,4,4,512]{4,3,1,2,0:T(4,128)(2,1)} copy(bf16[8,32,4,4,512]{4,0,2,1,3:T(8,128)(2,1)} %bitcast.29) | data formatting | bytes 8388608 | tf_op jit(solution)/shard_map/transpose | solution.py:25
  361.9 7.7 %reshape_reshape.3 = bf16[2,2,2,32,4,2048]{5,3,4,2,1,0:T(8,128)(2,1)} reshape(bf16[8,32,4,4,512]{4,3,1,2,0:T(4,128)(2,1)} %copy.116) | data formatting | bytes 8388608 | tf_op jit(solution)/shard_map/reshape;reshape | solution.py:28
  369.7 2.6 select_select_fusion
  372.3 5.3 %copy.117 = bf16[2,2,2,32,4,2048]{5,4,3,2,1,0:T(4,128)(2,1)} copy(bf16[2,2,2,32,4,2048]{5,3,4,2,1,0:T(8,128)(2,1)S(1)} %select_select_fusion) | data formatting | bytes 8388608
  377.6 1.9 all-to-all-done.1
  379.5 5.5 %multiply_reduce_fusion = f32[256,512]{1,0:T(8,128)S(1)} fusion(bf16[2048,512,1]{1,0,2:T(8,128)(2,1)} %bitcast.21, s32[256,6]{0,1:T(8,128)S(1)} %multiply_add_fusion, f32[256,6]{0,1:T(8,128)S(1)} %multiply_divide_fusion), kind=kOutput, calls=%fused_computation.22 | convolution fusion | flops 3225812992 | bytes 2633728 | tf_op jit(solution)/shard_map/dot_general | solution.py:120
  384.9 3.3 reduce-scatter.7.cloned.1.call-done
  388.3 1.7 add_convert_fusion
  (71 shorter events, 4.7 us)
Async XLA Ops:
  8.0 343.4 %copy-start = (bf16[2048,64]{0,1:T(8,128)(2,1)S(1)}, bf16[2048,64]{0,1:T(8,128)(2,1)}, u32[]{:S(2)}) copy-start(bf16[2048,64]{0,1:T(8,128)(2,1)} %param.11) | copy-start | bytes 786436
  8.0 7.6 %copy-start.11 = (s32[256,6]{0,1:T(8,128)S(1)}, s32[256,6]{0,1:T(8,128)}, u32[]{:S(2)}) copy-start(s32[256,6]{0,1:T(8,128)} %param.12) | copy-start | bytes 18436
  8.0 31.0 %all-gather.5.cloned.1.call-start = ((), (), s32[]{:S(2)}) async-start(), calls=%async_computation.8 | async-start | bytes 1572864 | tf_op jit(solution)/shard_map/all_gather | solution.py:69
  13.3 168.4 %all-gather.7.cloned.1.call-start = ((), (), s32[]{:S(2)}) async-start(), calls=%async_computation.9 | async-start | bytes 2162688 | tf_op jit(solution)/shard_map/all_gather | solution.py:45
  42.1 1.3 copy-start.2
  102.8 4.9 %copy-start.1 = (bf16[32,2,32,1024]{3,2,1,0:T(8,128)(2,1)}, bf16[32,2,32,1024]{3,2,1,0:T(8,128)(2,1)S(1)}, u32[]{:S(2)}) copy-start(bf16[32,2,32,1024]{3,2,1,0:T(8,128)(2,1)S(1)} %all_to_all.24) | copy-start | bytes 12582916
  102.8 4.7 %copy-start.9 = (bf16[2,64,704]{2,1,0:T(8,128)(2,1)S(1)}, bf16[2,64,704]{2,1,0:T(8,128)(2,1)}, u32[]{:S(2)}) copy-start(bf16[2,64,704]{2,1,0:T(8,128)(2,1)} %param.15) | copy-start | bytes 540676
  105.5 37.7 %collective-permute-start = (bf16[32,2,32,1024]{3,2,0,1:T(8,128)(2,1)}, bf16[32,2,32,1024]{3,2,0,1:T(8,128)(2,1)}, u32[]{:S(2)}, u32[]{:S(2)}) collective-permute-start(bf16[32,2,32,1024]{3,2,0,1:T(8,128)(2,1)} %copy.106), channel_id=1, source_target_pairs={{0,32},{32,0},{1,33},{33,1},{2,34},{34,2},{3,35},{35,3},{4,36},{36... | collective-permute-start | bytes 12582920 | tf_op jit(solution)/shard_map/ppermute | solution.py:101
  120.7 61.8 %reduce-scatter.9.cloned.1.call-start = ((), (), s32[]{:S(2)}) async-start(), calls=%async_computation.14 | async-start | bytes 12582912 | tf_op jit(solution)/shard_map/reduce_scatter | solution.py:39
  143.2 9.4 %copy-start.7 = (bf16[2,352,2048,1]{2,1,0,3:T(8,128)(2,1)S(1)}, bf16[2,352,2048,1]{2,1,0,3:T(8,128)(2,1)}, u32[]{:S(2)}) copy-start(bf16[2,352,2048,1]{2,1,0,3:T(8,128)(2,1)} %reshape.322) | copy-start | bytes 8650756
  162.2 0.9 copy-start.10
  162.3 20.7 %copy-start.3 = (bf16[256,2048]{1,0:T(8,128)(2,1)S(1)}, bf16[256,2048]{1,0:T(8,128)(2,1)}, u32[]{:S(2)}) copy-start(bf16[256,2048]{1,0:T(8,128)(2,1)} %copy-done.2) | copy-start | bytes 3145732
  162.3 77.7 %all-gather.11.cloned.1.call-start = ((), (), s32[]{:S(2)}) async-start(), calls=%async_computation.11 | async-start | bytes 3932160 | tf_op jit(solution)/shard_map/all_gather | solution.py:45
  181.7 151.0 %all-gather.9.cloned.1.call-start = ((), (), s32[]{:S(2)}) async-start(), calls=%async_computation.10 | async-start | bytes 7208960 | tf_op jit(solution)/shard_map/all_gather | solution.py:45
  182.3 157.4 %reduce-scatter.11.cloned.1.call-start = ((), (), s32[]{:S(2)}) async-start(), calls=%async_computation.15 | async-start | bytes 6291456 | tf_op jit(solution)/shard_map/reduce_scatter | solution.py:40
  189.3 42.1 %all-to-all-start.2 = ((bf16[128,4,2,512]{3,2,1,0:T(2,128)(2,1)}), bf16[128,4,2,512]{3,2,1,0:T(2,128)(2,1)S(1)}, u32[]{:S(2)}, u32[]{:S(2)}) async-start(bf16[128,4,2,512]{3,2,1,0:T(2,128)(2,1)} %bitcast.22), calls=%async_computation.6 | async-start | bytes 2097152 | tf_op jit(solution)/shard_map/all_to_all | solution.py:153
  207.8 30.5 %copy-start.12 = (s32[2]{0:T(128)S(1)}, s32[2]{0:T(128)}, u32[]{:S(2)}) copy-start(s32[2]{0:T(128)} %param.18) | copy-start | bytes 28
  231.5 1.0 copy-start.5
  232.4 110.5 %all-to-all-start.3 = ((bf16[8,1,512,512]{3,0,1,2:T(8,128)(2,1)}), bf16[8,1,512,512]{3,0,1,2:T(8,128)(2,1)}, u32[]{:S(2)}, u32[]{:S(2)}) async-start(bf16[8,1,512,512]{3,0,1,2:T(8,128)(2,1)} %copy.128), calls=%async_computation.7 | async-start | bytes 8388608 | tf_op jit(solution)/shard_map/all_to_all | solution.py:23
  238.3 131.4 %reduce-scatter.5.cloned.1.call-start = ((), (), s32[]{:S(2)}) async-start(), calls=%async_computation.12 | async-start | bytes 1572864 | tf_op jit(solution)/shard_map/reduce_scatter | solution.py:39
  251.0 86.4 %copy-start.8 = (bf16[704,2048]{1,0:T(8,128)(2,1)S(1)}, bf16[704,2048]{1,0:T(8,128)(2,1)}, u32[]{:S(2)}) copy-start(bf16[704,2048]{1,0:T(8,128)(2,1)} %reshape.308) | copy-start | bytes 8650756
  339.6 11.8 %copy-start.4 = (bf16[256,2048]{1,0:T(8,128)(2,1)S(1)}, bf16[256,2048]{1,0:T(8,128)(2,1)}, u32[]{:S(2)}) copy-start(bf16[256,2048]{1,0:T(8,128)(2,1)} %copy-done.2) | copy-start | bytes 3145732
  339.6 12.4 %copy-start.6 = (bf16[128,4,2,512]{3,2,1,0:T(2,128)(2,1)S(1)}, bf16[128,4,2,512]{3,2,1,0:T(2,128)(2,1)}, u32[]{:S(2)}) copy-start(bf16[128,4,2,512]{3,2,1,0:T(2,128)(2,1)} %copy-done.5) | copy-start | bytes 3145732
  343.0 36.5 %all-to-all-start.1 = ((bf16[32,2,32,512]{3,2,1,0:T(8,128)(2,1)}), bf16[32,2,32,512]{3,2,1,0:T(8,128)(2,1)}, u32[]{:S(2)}, u32[]{:S(2)}) async-start(bf16[32,2,32,512]{3,2,1,0:T(8,128)(2,1)} %copy.109), calls=%async_computation.5 | async-start | bytes 4194304 | tf_op jit(solution)/shard_map/all_to_all | solution.py:116
  351.3 37.0 %reduce-scatter.7.cloned.1.call-start = ((), (), s32[]{:S(2)}) async-start(), calls=%async_computation.13 | async-start | bytes 786432 | tf_op jit(solution)/shard_map/reduce_scatter | solution.py:40
Sparse Core Ops, SparseCore 0:
  13.4 25.5 all-gather.4
  162.4 18.6 reduce-scatter.8
  185.5 87.1 reduce-scatter.10
  339.6 11.4 reduce-scatter.4
  369.8 18.4 reduce-scatter.6
Sparse Core Ops, SparseCore 1:
  120.8 28.9 all-gather.6
  181.8 54.0 all-gather.10
  237.3 95.3 all-gather.8

commit v2 on v1

--- a/solution.py
+++ b/solution.py
@@ -35,9 +35,19 @@
     return jnp.swapaxes(split, dim, dim + 1).reshape(shape)
 
 
-def row_reduce_scatter(x, dim):
-    half = lax.psum_scatter(x, "core", scatter_dimension=dim, tiled=True)
-    return lax.psum_scatter(half, "xl", scatter_dimension=dim, tiled=True)
+def swap_gather(x, name, index):
+    other = lax.ppermute(x, name, perm=[(0, 1), (1, 0)])
+    return jnp.where(
+        index == 0, jnp.concatenate([x, other], axis=-1), jnp.concatenate([other, x], axis=-1)
+    )
+
+
+def swap_reduce(x, name, index, dim):
+    block = x.shape[dim] // 2
+    keep = lax.dynamic_slice_in_dim(x, index * block, block, axis=dim)
+    give = lax.dynamic_slice_in_dim(x, (1 - index) * block, block, axis=dim)
+    got = lax.ppermute(give, name, perm=[(0, 1), (1, 0)])
+    return keep.astype(jnp.float32) + got.astype(jnp.float32)
 
 
 def col_gather(x, dim):
@@ -65,8 +75,9 @@
     core_index = lax.axis_index("core")
     tok_rows = tokens.shape[0]
     slice_width = tokens.shape[1]
-    gathered = lax.all_gather(tokens, "core", axis=1, tiled=True)
-    gathered = lax.all_gather(gathered, "xl", axis=1, tiled=True)
+    xl_index = lax.axis_index("xl")
+    gathered = swap_gather(tokens, "core", core_index)
+    gathered = swap_gather(gathered, "xl", xl_index)
     width = gathered.shape[1]
     half_width = width // 2
     tokens_f = gathered.astype(jnp.float32)
@@ -112,10 +123,12 @@
     partial_out = jnp.einsum(
         "secf,efd->secd", hidden, row_order(expert_out, 2), preferred_element_type=jnp.float32
     )
-    summed = row_reduce_scatter(partial_out.astype(jnp.bfloat16), 3)
-    returned = lax.all_to_all(summed, COL, split_axis=0, concat_axis=0, tiled=True).reshape(
-        slot_total, slice_width
-    )
+    chip_sum = swap_reduce(partial_out.astype(jnp.bfloat16), "core", core_index, 3)
+    send = chip_sum.astype(jnp.bfloat16).reshape(col_count, local_experts, CAP, 2, slice_width)
+    send = send.transpose(3, 0, 1, 2, 4).reshape(2 * col_count, local_experts, CAP, slice_width)
+    both = lax.all_to_all(send, ("xl",) + COL, split_axis=0, concat_axis=0, tiled=True)
+    both = both.astype(jnp.float32).reshape(2, slot_total, slice_width)
+    returned = (both[0] + both[1]).astype(jnp.bfloat16)
     pick = (dest_index[:, None] == slots[None, :]).astype(jnp.bfloat16)
     routed = jnp.dot(pick, returned, preferred_element_type=jnp.float32)
     routed = routed.reshape(tok_rows, top_count, slice_width)
@@ -132,7 +145,8 @@
         row_order(col_gather(shared_out, 1), 1),
         preferred_element_type=jnp.float32,
     )
-    shared_part = row_reduce_scatter(shared_terms.astype(jnp.bfloat16), 1).astype(jnp.float32)
+    shared_half = swap_reduce(shared_terms.astype(jnp.bfloat16), "core", core_index, 1)
+    shared_part = swap_reduce(shared_half.astype(jnp.bfloat16), "xl", xl_index, 1)
     mixed_out = (shared_part + routed_sum).astype(jnp.bfloat16)
     layers = kv_cache.shape[0]
     pairs = kv_cache.shape[1]

time: 405 us -> 386 us (0.953)
  the two profiles are of different devices: /device:TPU:1 before, /device:TPU:80 now
where the time goes in v2:
time: 386 us; the launch traced here: 379 us
  blocking collectives  86.3 us (22%)
  waiting for transfers between devices  82.9 us (21%)
  local copies, waits for them, and re-layouts  81.7 us (21%)
  starting transfers between devices  51.2 us (13%)
  matrix products  42.2 us (11%)
  other arithmetic  19.9 us (5%)
  between operations  14.7 us (4%)
    all_gather x3, blocking collectives, col_gather(): x = lax.all_gather(x, name, axis=dim, tiled=True)  86.3 us
    all_gather x3, waiting for transfers between devices, col_gather(): x = lax.all_gather(x, name, axis=dim, tiled=True)  38.6 us
    all_to_all x1, waiting for transfers between devices, relay_slabs(): lax.all_to_all(sectioned, AXES, split_axis=2, concat_axis=1, tiled=True)  34.1 us
    all_to_all x1, starting transfers between devices, local(): lax.all_to_all(outbound, AXES, split_axis=0, concat_axis=0, tiled=True)  15.4 us
    reshape x2, local copies, waits for them, and re-layouts, local(): chip_sum.astype(jnp.bfloat16)  13 us
    all_to_all x1, starting transfers between devices, local(): lax.all_to_all(send, ('xl',) + COL, split_axis=0, concat_axis=0, tiled=True)  11.4 us
    unnamed x29, local copies, waits for them, and re-layouts  11.2 us
    reshape x2, local copies, waits for them, and re-layouts, row_order(): split = x.reshape(shape[:dim] + (2, 2, quarter) + shape[dim + 1:])  10.9 us
  transfers between devices with their start and end apart: 13, of which 4 were waited for; matrix products, arithmetic and copies ran while one was open for 35% of the time, Pallas kernels for 0%

profile of v2, /device:TPU:80, one launch (start us, length us, event | category | flops | bytes accessed | tf_op | source)
XLA Modules:
  0.0 379.0 jit_solution(8421206254680446549)
XLA Ops:
  7.3 0.8 copy.103
  9.0 1.2 maximum_select_fusion.1
  10.2 1.6 collective-permute-start.1
  11.8 1.0 fusion.36
  13.1 2.3 fusion.3
  15.3 8.9 %collective-permute-done.1 = bf16[256,1024]{1,0:T(8,128)(2,1)S(1)} collective-permute-done((bf16[256,1024]{1,0:T(8,128)(2,1)S(1)}, bf16[256,1024]{1,0:T(8,128)(2,1)S(1)}, u32[]{:S(2)}, u32[]{:S(2)}) %collective-permute-start.1) | collective-permute-done | bytes 524320 | tf_op jit(solution)/shard_map/ppermute | solution.py:39
  24.9 1.0 copy-done.3
  25.9 3.3 convolution_convert_fusion.1
  29.2 10.2 %all-to-all-start = ((bf16[32,2,32,1024]{3,2,1,0:T(8,128)(2,1)}), bf16[32,2,32,1024]{3,2,1,0:T(8,128)(2,1)}, u32[]{:S(2)}, u32[]{:S(2)}) async-start(bf16[32,2,32,1024]{3,2,1,0:T(8,128)(2,1)} %bitcast.100), calls=%async_computation | async-start | bytes 8388608 | tf_op jit(solution)/shard_map/all_to_all | solution.py:111
  39.6 55.4 %all_gather.18 = bf16[2,256,704]{2,0,1:T(2,128)(2,1)S(1)} all-gather(bf16[2,64,704]{2,0,1:T(2,128)(2,1)S(1)} %copy.100), channel_id=1, replica_groups=mesh['xl'=2,'core'=2,'y'=4,'xh'=2,'z'=4] {'z'}, dimensions={1}, use_global_device_ids=true | all-gather | bytes 901120 | tf_op jit(solution)/shard_map/all_gather | solution.py:55
  95.0 1.9 copy.101
  97.0 12.5 %all_gather.21 = bf16[704,256]{0,1:T(8,128)(2,1)S(1)} all-gather(bf16[704,64]{0,1:T(8,128)(2,1)S(1)} %copy-done.10), channel_id=1, replica_groups=mesh['xl'=2,'core'=2,'y'=4,'xh'=2,'z'=4] {'z'}, dimensions={1}, use_global_device_ids=true | all-gather | bytes 450560 | tf_op jit(solution)/shard_map/all_gather | solution.py:55
  109.5 18.5 %all_gather.22 = bf16[704,512]{0,1:T(8,128)(2,1)} all-gather(bf16[704,256]{0,1:T(8,128)(2,1)S(1)} %all_gather.21), channel_id=1, replica_groups=mesh['xl'=2,'core'=2,'y'=4,'xh'=2,'z'=4] {'xh'}, dimensions={1}, use_global_device_ids=true | all-gather | bytes 1081344 | tf_op jit(solution)/shard_map/all_gather | solution.py:55
  128.0 5.2 %copy.106 = bf16[32,2,32,1024]{3,2,0,1:T(8,128)(2,1)} copy(bf16[32,2,32,1024]{3,2,1,0:T(8,128)(2,1)} %all-to-all-done) | data formatting | bytes 8388608 | tf_op jit(solution)/shard_map/all_to_all | solution.py:111
  133.6 3.3 reshape.319
  137.0 4.8 %copy.108 = bf16[2,352,2,2,512]{4,3,2,1,0:T(2,128)(2,1)S(1)} copy(bf16[2,352,2,2,512]{4,2,3,1,0:T(2,128)(2,1)} %bitcast.103) | data formatting | bytes 5767168 | tf_op jit(solution)/shard_map/transpose | solution.py:35
  141.7 3.4 reshape.332
  145.1 3.8 fusion.33
  148.9 1.5 broadcast_in_dim.44
  150.4 1.3 copy_dynamic-update-slice_fusion
  151.7 15.4 %all-to-all-start.2 = ((bf16[128,4,2,512]{3,2,1,0:T(2,128)(2,1)}), bf16[128,4,2,512]{3,2,1,0:T(2,128)(2,1)S(1)}, u32[]{:S(2)}, u32[]{:S(2)}) async-start(bf16[128,4,2,512]{3,2,1,0:T(2,128)(2,1)} %bitcast.25), calls=%async_computation.2 | async-start | bytes 2097152 | tf_op jit(solution)/shard_map/all_to_all | solution.py:167
  167.8 6.3 %fusion.10 = f32[2,2,352,32,32]{2,4,3,1,0:T(8,128)S(1)} fusion(bf16[2,2,2048,352]{2,3,1,0:T(8,128)(2,1)} %param.13, s32[]{:T(128)S(6)} %select_n.85, bf16[32,2,32,1024]{3,2,1,0:T(8,128)(2,1)} %all-to-all-done), kind=kOutput, calls=%fused_computation.16 | convolution fusion | flops 2952790016 | bytes 12845060 | tf_op jit(solution)/shard_map/secd,egdf->gsecf/dot_general | solution.py:117
  174.1 9.2 %add_bitcast_fusion = f32[2,32,2,32,352]{4,3,1,0,2:T(8,128)} fusion(f32[2,2,352,32,32]{2,4,3,1,0:T(8,128)S(1)} %fusion.10, bf16[32,2,32,1024]{3,2,0,1:T(8,128)(2,1)} %collective-permute-done.4, bf16[2,2,2048,352]{2,3,1,0:T(8,128)(2,1)} %param.13, s32[]{:T(128)S(6)} %select_n.86), kind=kOutput, calls=%fused_computation.9 | convolution fusion | flops 2954231808 | bytes 18612228 | tf_op jit(solution)/shard_map/secd,egdf->gsecf/dot_general | solution.py:119
  183.3 8.2 %convolution_convert_fusion = bf16[2,32,32,2048]{3,2,1,0:T(8,128)(2,1)S(1)} fusion(bf16[2,352,2048,1]{2,1,0,3:T(8,128)(2,1)} %reshape.332, f32[2,32,2,32,352]{4,3,1,0,2:T(8,128)} %add_bitcast_fusion), kind=kOutput, calls=%fused_computation.11 | convolution fusion | flops 2961309696 | bytes 17039360 | tf_op jit(solution)/shard_map/secf,efd->secd/dot_general | solution.py:123
  191.5 2.7 dynamic-slice_bitcast_fusion
  194.3 2.8 copy-done.2
  197.2 4.4 %copy.128 = bf16[8,1,512,512]{3,0,1,2:T(8,128)(2,1)} copy(bf16[8,1,512,512]{3,2,0,1:T(8,128)(2,1)S(1)} %bitcast.104) | data formatting | bytes 8388608 | tf_op jit(solution)/shard_map/reshape | solution.py:21
  201.6 10.7 %all-to-all-start.3 = ((bf16[8,1,512,512]{3,0,1,2:T(8,128)(2,1)}), bf16[8,1,512,512]{3,0,1,2:T(8,128)(2,1)}, u32[]{:S(2)}, u32[]{:S(2)}) async-start(bf16[8,1,512,512]{3,0,1,2:T(8,128)(2,1)} %copy.128), calls=%async_computation.3 | async-start | bytes 8388608 | tf_op jit(solution)/shard_map/all_to_all | solution.py:23
  214.0 8.0 %fusion.5 = bf16[32,2,32,1024]{3,2,0,1:T(8,128)(2,1)} fusion(bf16[32,2,32,1024]{3,2,0,1:T(8,128)(2,1)} %collective-permute-done.5, bf16[2,32,32,2048]{3,2,1,0:T(8,128)(2,1)} %copy-done.2, s32[]{:T(128)S(6)} %select_n.85), kind=kLoop, calls=%fused_computation.8 | loop fusion | flops 8388608 | bytes 12582916 | tf_op jit(solution)/shard_map/convert_element_type | solution.py:127
  222.0 7.8 %reshape.321 = bf16[32,2,32,2,512]{4,3,2,0,1:T(2,128)(2,1)} reshape(bf16[32,2,32,1024]{3,2,0,1:T(8,128)(2,1)} %fusion.5) | data formatting | bytes 8388608 | tf_op jit(solution)/shard_map/reshape | solution.py:127
  229.8 5.2 %copy.109 = bf16[32,2,32,2,512]{4,2,1,0,3:T(8,128)(2,1)} copy(bf16[32,2,32,2,512]{4,3,2,0,1:T(2,128)(2,1)} %reshape.321) | data formatting | bytes 8388608 | tf_op jit(solution)/shard_map/reshape | solution.py:127
  235.0 34.1 %all-to-all-done.3 = bf16[8,1,512,512]{3,0,1,2:T(8,128)(2,1)} async-done(((bf16[8,1,512,512]{3,0,1,2:T(8,128)(2,1)}), bf16[8,1,512,512]{3,0,1,2:T(8,128)(2,1)}, u32[]{:S(2)}, u32[]{:S(2)}) %all-to-all-start.3) | async-done | bytes 4194336 | tf_op jit(solution)/shard_map/all_to_all | solution.py:23
  269.1 11.4 %all-to-all-start.1 = ((bf16[64,2,32,512]{3,2,1,0:T(8,128)(2,1)}), bf16[64,2,32,512]{3,2,1,0:T(8,128)(2,1)}, u32[]{:S(2)}, u32[]{:S(2)}) async-start(bf16[64,2,32,512]{3,2,1,0:T(8,128)(2,1)} %bitcast.101), calls=%async_computation.1 | async-start | bytes 8388608 | tf_op jit(solution)/shard_map/all_to_all | solution.py:129
  281.9 0.8 copy.114
  282.7 1.6 convert_element_type.137
  284.3 7.4 %copy.116 = bf16[8,32,4,4,512]{4,3,1,2,0:T(4,128)(2,1)} copy(bf16[8,32,4,4,512]{4,0,2,1,3:T(8,128)(2,1)} %bitcast.32) | data formatting | bytes 8388608 | tf_op jit(solution)/shard_map/transpose | solution.py:25
  291.7 7.8 %reshape_reshape.3 = bf16[2,2,2,32,4,2048]{5,3,4,2,1,0:T(8,128)(2,1)} reshape(bf16[8,32,4,4,512]{4,3,1,2,0:T(4,128)(2,1)} %copy.116) | data formatting | bytes 8388608 | tf_op jit(solution)/shard_map/reshape;reshape | solution.py:28
  299.5 7.6 %copy.102 = bf16[704,2,2,512]{3,1,2,0:T(2,128)(2,1)S(1)} copy(bf16[704,2,2,512]{0,3,2,1:T(8,128)(2,1)} %bitcast.106) | data formatting | bytes 5767168 | tf_op jit(solution)/shard_map/reshape | solution.py:34
  307.1 3.3 reshape.317
  310.4 38.6 %all-gather.6.cloned.1.call-done = bf16[2,2048,704]{1,2,0:T(8,128)(2,1)} async-done(((bf16[2,512,704]{1,2,0:T(8,128)(2,1)}), bf16[2,2048,704]{1,2,0:T(8,128)(2,1)}) %all-gather.6.cloned.1.call-update) | async-done | bytes 5767184 | tf_op jit(solution)/shard_map/all_gather | solution.py:55
  349.0 4.7 %convolution_bitcast_fusion = f32[2,256,704]{1,2,0:T(8,128)S(1)} fusion(bf16[2,2048,704]{1,2,0:T(8,128)(2,1)} %all-gather.6.cloned.1.call-done, bf16[256,2048]{1,0:T(8,128)(2,1)} %copy-done.3), kind=kOutput, calls=%fused_computation.41 | convolution fusion | flops 1476395008 | bytes 8257536 | tf_op jit(solution)/shard_map/td,gdf->gtf/dot_general | solution.py:136
  353.8 1.1 convolution_convert_fusion.2
  356.2 0.8 select_select_fusion
  357.0 5.3 %copy.117 = bf16[2,2,2,32,4,2048]{5,4,3,2,1,0:T(4,128)(2,1)} copy(bf16[2,2,2,32,4,2048]{5,3,4,2,1,0:T(8,128)(2,1)S(1)} %select_select_fusion) | data formatting | bytes 8388608
  363.3 3.4 convert_element_type.128
  366.7 0.8 fusion.7
  367.5 3.7 multiply_reduce_fusion
  371.2 0.8 add_convert_fusion.1
  (75 shorter events, 8.8 us)
Async XLA Ops:
  7.2 273.5 %copy-start = (bf16[2048,64]{0,1:T(8,128)(2,1)S(1)}, bf16[2048,64]{0,1:T(8,128)(2,1)}, u32[]{:S(2)}) copy-start(bf16[2048,64]{0,1:T(8,128)(2,1)} %param.11) | copy-start | bytes 786436
  7.2 5.9 %copy-start.11 = (s32[256,6]{0,1:T(8,128)S(1)}, s32[256,6]{0,1:T(8,128)}, u32[]{:S(2)}) copy-start(s32[256,6]{0,1:T(8,128)} %param.12) | copy-start | bytes 18436
  7.2 1.8 collective-permute-start
  10.2 14.0 %collective-permute-start.1 = (bf16[256,1024]{1,0:T(8,128)(2,1)S(1)}, bf16[256,1024]{1,0:T(8,128)(2,1)S(1)}, u32[]{:S(2)}, u32[]{:S(2)}) collective-permute-start(bf16[256,1024]{1,0:T(8,128)(2,1)S(1)} %maximum_select_fusion.1), channel_id=1, source_target_pairs={{0,64},{64,0},{1,65},{65,1},{2,66},{66,2},{3,67},{67,3},{4,68},{68... | collective-permute-start | bytes 1572872 | tf_op jit(solution)/shard_map/ppermute | solution.py:39
  24.9 1.0 copy-start.3
  29.2 10.2 %copy-start.9 = (bf16[2,64,704]{2,1,0:T(8,128)(2,1)S(1)}, bf16[2,64,704]{2,1,0:T(8,128)(2,1)}, u32[]{:S(2)}) copy-start(bf16[2,64,704]{2,1,0:T(8,128)(2,1)} %param.15) | copy-start | bytes 540676
  29.2 67.8 %copy-start.10 = (bf16[704,64]{0,1:T(8,128)(2,1)S(1)}, bf16[704,64]{0,1:T(8,128)(2,1)}, u32[]{:S(2)}) copy-start(bf16[704,64]{0,1:T(8,128)(2,1)} %param.16) | copy-start | bytes 270340
  29.2 98.8 %all-to-all-start = ((bf16[32,2,32,1024]{3,2,1,0:T(8,128)(2,1)}), bf16[32,2,32,1024]{3,2,1,0:T(8,128)(2,1)}, u32[]{:S(2)}, u32[]{:S(2)}) async-start(bf16[32,2,32,1024]{3,2,1,0:T(8,128)(2,1)} %bitcast.100), calls=%async_computation | async-start | bytes 8388608 | tf_op jit(solution)/shard_map/all_to_all | solution.py:111
  39.3 128.0 %all-gather.4.cloned.1.call-start = ((), (), s32[]{:S(2)}) async-start(), calls=%async_computation.4 | async-start | bytes 2162688 | tf_op jit(solution)/shard_map/all_gather | solution.py:55
  96.9 202.6 %all-gather.8.cloned.1.call-start = ((), (), s32[]{:S(2)}) async-start(), calls=%async_computation.6 | async-start | bytes 3932160 | tf_op jit(solution)/shard_map/all_gather | solution.py:55
  128.0 5.7 %copy-start.7 = (bf16[2,352,2048]{2,1,0:T(8,128)(2,1)S(1)}, bf16[2,352,2048]{2,1,0:T(8,128)(2,1)}, u32[]{:S(2)}) copy-start(bf16[2,352,2048]{2,1,0:T(8,128)(2,1)} %param.14) | copy-start | bytes 8650756
  133.1 41.0 %collective-permute-start.4 = (bf16[32,2,32,1024]{3,2,0,1:T(8,128)(2,1)}, bf16[32,2,32,1024]{3,2,0,1:T(8,128)(2,1)}, u32[]{:S(2)}, u32[]{:S(2)}) collective-permute-start(bf16[32,2,32,1024]{3,2,0,1:T(8,128)(2,1)} %copy.106), channel_id=1, source_target_pairs={{0,32},{32,0},{1,33},{33,1},{2,34},{34,2},{3,35},{35,3},{4,36},{36... | collective-permute-start | bytes 12582920 | tf_op jit(solution)/shard_map/ppermute | solution.py:112
  151.7 49.9 %all-to-all-start.2 = ((bf16[128,4,2,512]{3,2,1,0:T(2,128)(2,1)}), bf16[128,4,2,512]{3,2,1,0:T(2,128)(2,1)S(1)}, u32[]{:S(2)}, u32[]{:S(2)}) async-start(bf16[128,4,2,512]{3,2,1,0:T(2,128)(2,1)} %bitcast.25), calls=%async_computation.2 | async-start | bytes 2097152 | tf_op jit(solution)/shard_map/all_to_all | solution.py:167
  167.1 181.9 %all-gather.6.cloned.1.call-start = ((), (), s32[]{:S(2)}) async-start(), calls=%async_computation.5 | async-start | bytes 7208960 | tf_op jit(solution)/shard_map/all_gather | solution.py:55
  191.5 5.6 %copy-start.2 = (bf16[2,32,32,2048]{3,2,1,0:T(8,128)(2,1)}, bf16[2,32,32,2048]{3,2,1,0:T(8,128)(2,1)S(1)}, u32[]{:S(2)}) copy-start(bf16[2,32,32,2048]{3,2,1,0:T(8,128)(2,1)S(1)} %convolution_convert_fusion) | copy-start | bytes 25165828
  191.5 5.7 %copy-start.5 = (bf16[2,2,2,1,512,512]{5,4,3,2,1,0:T(8,128)(2,1)S(1)}, bf16[2,2,2,1,512,512]{5,4,3,2,1,0:T(8,128)(2,1)}, u32[]{:S(2)}) copy-start(bf16[2,2,2,1,512,512]{5,4,3,2,1,0:T(8,128)(2,1)} %param.17) | copy-start | bytes 12582916
  197.1 16.9 %collective-permute-start.5 = (bf16[32,2,32,1024]{3,2,0,1:T(8,128)(2,1)}, bf16[32,2,32,1024]{3,2,0,1:T(8,128)(2,1)}, u32[]{:S(2)}, u32[]{:S(2)}) collective-permute-start(bf16[32,2,32,1024]{3,2,0,1:T(8,128)(2,1)} %dynamic-slice_bitcast_fusion), channel_id=1, source_target_pairs={{0,32},{32,0},{1,33},{33,1},{2,34},{34,2},{3,35},{35,3},{4,36},{36... | collective-permute-start | bytes 12582920 | tf_op jit(solution)/shard_map/ppermute | solution.py:49
  201.6 10.7 %copy-start.12 = (s32[2]{0:T(128)S(1)}, s32[2]{0:T(128)}, u32[]{:S(2)}) copy-start(s32[2]{0:T(128)} %param.18) | copy-start | bytes 28
  201.6 67.5 %all-to-all-start.3 = ((bf16[8,1,512,512]{3,0,1,2:T(8,128)(2,1)}), bf16[8,1,512,512]{3,0,1,2:T(8,128)(2,1)}, u32[]{:S(2)}, u32[]{:S(2)}) async-start(bf16[8,1,512,512]{3,0,1,2:T(8,128)(2,1)} %copy.128), calls=%async_computation.3 | async-start | bytes 8388608 | tf_op jit(solution)/shard_map/all_to_all | solution.py:23
  269.1 11.6 %copy-start.4 = (bf16[256,2048]{1,0:T(8,128)(2,1)S(1)}, bf16[256,2048]{1,0:T(8,128)(2,1)}, u32[]{:S(2)}) copy-start(bf16[256,2048]{1,0:T(8,128)(2,1)} %copy-done.3) | copy-start | bytes 3145732
  269.1 94.2 %all-to-all-start.1 = ((bf16[64,2,32,512]{3,2,1,0:T(8,128)(2,1)}), bf16[64,2,32,512]{3,2,1,0:T(8,128)(2,1)}, u32[]{:S(2)}, u32[]{:S(2)}) async-start(bf16[64,2,32,512]{3,2,1,0:T(8,128)(2,1)} %bitcast.101), calls=%async_computation.1 | async-start | bytes 8388608 | tf_op jit(solution)/shard_map/all_to_all | solution.py:129
  310.4 43.3 %copy-start.8 = (bf16[704,2048]{1,0:T(8,128)(2,1)S(1)}, bf16[704,2048]{1,0:T(8,128)(2,1)}, u32[]{:S(2)}) copy-start(bf16[704,2048]{1,0:T(8,128)(2,1)} %reshape.317) | copy-start | bytes 8650756
  353.7 2.2 copy-start.1
  353.7 2.5 copy-start.6
  354.9 7.4 %collective-permute-start.2 = (bf16[256,1024]{1,0:T(8,128)(2,1)S(1)}, bf16[256,1024]{1,0:T(8,128)(2,1)S(1)}, u32[]{:S(2)}, u32[]{:S(2)}) collective-permute-start(bf16[256,1024]{1,0:T(8,128)(2,1)S(1)} %constant_dynamic-slice_fusion.1), channel_id=1, source_target_pairs={{0,32},{32,0},{1,33},{33,1},{2,34},{34,2},{3,35},{35,3},{4,36},{36... | collective-permute-start | bytes 1572872 | tf_op jit(solution)/shard_map/ppermute | solution.py:49
  362.5 8.6 %collective-permute-start.3 = (bf16[256,512]{1,0:T(8,128)(2,1)S(1)}, bf16[256,512]{1,0:T(8,128)(2,1)S(1)}, u32[]{:S(2)}, u32[]{:S(2)}) collective-permute-start(bf16[256,512]{1,0:T(8,128)(2,1)S(1)} %constant_dynamic-slice_fusion), channel_id=1, source_target_pairs={{0,64},{64,0},{1,65},{65,1},{2,66},{66,2},{3,67},{67,3},{4,68},{68... | collective-permute-start | bytes 786440 | tf_op jit(solution)/shard_map/ppermute | solution.py:49
Sparse Core Ops, SparseCore 0:
  97.1 38.7 all-gather.3
  137.5 52.6 all-gather.7
  191.8 157.1 all-gather.5

commit v3 on v2

--- a/solution.py
+++ b/solution.py
@@ -50,10 +50,26 @@
     return keep.astype(jnp.float32) + got.astype(jnp.float32)
 
 
-def col_gather(x, dim):
-    for name in ("z", "xh", "y"):
-        x = lax.all_gather(x, name, axis=dim, tiled=True)
-    return x
+def ring_gather(x, name, size):
+    if size == 2:
+        return jnp.stack([x, lax.ppermute(x, name, perm=[(0, 1), (1, 0)])], axis=0)
+    half = x.shape[0] // 2
+    fwd, bwd = x[:half], x[half:]
+    ahead = [(i, (i + 1) % size) for i in range(size)]
+    behind = [(i, (i - 1) % size) for i in range(size)]
+    fwd_parts, bwd_parts = [fwd], [bwd]
+    for _ in range(1, size):
+        fwd = lax.ppermute(fwd, name, perm=ahead)
+        bwd = lax.ppermute(bwd, name, perm=behind)
+        fwd_parts.append(fwd)
+        bwd_parts.append(bwd)
+    return jnp.stack(
+        [
+            jnp.concatenate([fwd_parts[d], bwd_parts[(size - d) % size]], axis=0)
+            for d in range(size)
+        ],
+        axis=0,
+    )
 
 
 def local(
@@ -133,18 +149,46 @@
     routed = jnp.dot(pick, returned, preferred_element_type=jnp.float32)
     routed = routed.reshape(tok_rows, top_count, slice_width)
     routed_sum = jnp.sum(gate_weights[:, :, None] * routed, axis=1)
+    rows_each = shared_in.shape[1]
+    stacked = jnp.concatenate(
+        [shared_in.transpose(1, 0, 2), shared_out.T[:, None, :]], axis=1
+    )
+    sizes = {name: lax.axis_size(name) for name in COL}
+    ring = ring_gather(stacked, "z", sizes["z"])
+    ring = ring_gather(ring, "xh", sizes["xh"])
+    ring = ring_gather(ring, "y", sizes["y"])
+    ring = ring.reshape(col_count, rows_each, 3, ring.shape[-1])
+    offsets = jnp.arange(col_count, dtype=jnp.int32)
+    d_y = offsets // (sizes["xh"] * sizes["z"])
+    d_xh = (offsets // sizes["z"]) % sizes["xh"]
+    d_z = offsets % sizes["z"]
+    me_y = lax.axis_index("y")
+    me_xh = lax.axis_index("xh")
+    me_z = lax.axis_index("z")
+    source_col = (
+        ((me_y - d_y) % sizes["y"]) * (sizes["xh"] * sizes["z"])
+        + ((me_xh - d_xh) % sizes["xh"]) * sizes["z"]
+        + (me_z - d_z) % sizes["z"]
+    )
+    normed_ring = jnp.take(normed.reshape(tok_rows, col_count, rows_each), source_col, axis=1)
     shared_acc = jnp.einsum(
-        "td,gdf->gtf",
-        normed,
-        col_gather(shared_in, 1),
-        preferred_element_type=jnp.float32,
+        "tcj,cjgs->gts", normed_ring, ring[:, :, 0:2, :], preferred_element_type=jnp.float32
     )
     shared_hidden = (jax.nn.silu(shared_acc[0]) * shared_acc[1]).astype(jnp.bfloat16)
-    shared_terms = jnp.dot(
-        shared_hidden,
-        row_order(col_gather(shared_out, 1), 1),
-        preferred_element_type=jnp.float32,
-    )
+    terms_ring = jnp.einsum(
+        "ts,cjs->tcj", shared_hidden, ring[:, :, 2, :], preferred_element_type=jnp.float32
+    )
+    cols = jnp.arange(col_count, dtype=jnp.int32)
+    c_y = cols // (sizes["xh"] * sizes["z"])
+    c_xh = (cols // sizes["z"]) % sizes["xh"]
+    c_z = cols % sizes["z"]
+    ring_of_col = (
+        ((me_y - c_y) % sizes["y"]) * (sizes["xh"] * sizes["z"])
+        + ((me_xh - c_xh) % sizes["xh"]) * sizes["z"]
+        + (me_z - c_z) % sizes["z"]
+    )
+    shared_terms = jnp.take(terms_ring, ring_of_col, axis=1).reshape(tok_rows, width)
+    shared_terms = row_order(shared_terms, 1)
     shared_half = swap_reduce(shared_terms.astype(jnp.bfloat16), "core", core_index, 1)
     shared_part = swap_reduce(shared_half.astype(jnp.bfloat16), "xl", xl_index, 1)
     mixed_out = (shared_part + routed_sum).astype(jnp.bfloat16)

time: 386 us -> 414 us (1.073)
  the two profiles are of different devices: /device:TPU:80 before, /device:TPU:1 now
where the time goes in v3:
time: 414 us; the launch traced here: 406 us
  waiting for transfers between devices  119 us (29%)
  local copies, waits for them, and re-layouts  85.5 us (21%)
  blocking collectives  60.6 us (15%)
  starting transfers between devices  55.6 us (13%)
  matrix products  43.2 us (10%)
  other arithmetic  40.4 us (10%)
    ppermute x1, waiting for transfers between devices, ring_gather(): return jnp.stack([x, lax.ppermute(x, name, perm=[(0, 1), (1, 0)])], axis=0)  65.5 us
    all_to_all x1, blocking collectives, local(): lax.all_to_all(outgoing, COL, split_axis=0, concat_axis=0, tiled=True)  60.6 us
    ppermute x6, waiting for transfers between devices, ring_gather(): bwd = lax.ppermute(bwd, name, perm=behind)  45.3 us
    another operation x9, other arithmetic, ring_gather(): jnp.stack([jnp.concatenate([fwd_parts[d], bwd_parts[(size - d) % size]],...  17.6 us
    ppermute x6, starting transfers between devices, ring_gather(): bwd = lax.ppermute(bwd, name, perm=behind)  15.4 us
    reshape x2, local copies, waits for them, and re-layouts, local(): chip_sum.astype(jnp.bfloat16)  13 us
    unnamed x49, local copies, waits for them, and re-layouts  12.8 us
    all_to_all x1, starting transfers between devices, relay_slabs(): lax.all_to_all(sectioned, AXES, split_axis=2, concat_axis=1, tiled=True)  9.94 us
  transfers between devices with their start and end apart: 22, of which 5 were waited for; matrix products, arithmetic and copies ran while one was open for 39% of the time, Pallas kernels for 0%

profile of v3, /device:TPU:1, one launch (start us, length us, event | category | flops | bytes accessed | tf_op | source)
XLA Modules:
  0.0 406.3 jit_solution(3232636880221341495)
XLA Ops:
  8.0 2.3 fusion.3
  10.3 8.2 %collective-permute-done.14 = bf16[256,1024]{0,1:T(8,128)(2,1)S(1)} collective-permute-done((bf16[256,1024]{0,1:T(8,128)(2,1)S(1)}, bf16[256,1024]{0,1:T(8,128)(2,1)S(1)}, u32[]{:S(2)}, u32[]{:S(2)}) %collective-permute-start.14) | collective-permute-done | bytes 524320 | tf_op jit(solution)/shard_map/ppermute | solution.py:39
  20.6 60.6 %all_to_all.24 = bf16[32,2,32,1024]{3,2,1,0:T(8,128)(2,1)S(1)} all-to-all(bf16[32,2,32,1024]{3,2,1,0:T(8,128)(2,1)S(1)} %bitcast.143), channel_id=1, replica_groups=mesh['xl'=2,'core'=2,'y'=4,'xh'=2,'z'=4] {'y','xh','z'}, dimensions={0} | all-to-all | bytes 8388608 | tf_op jit(solution)/shard_map/all_to_all | solution.py:127
  81.2 2.5 copy.128
  85.1 2.4 collective-permute-start.17
  89.9 3.4 reshape.581
  93.3 4.8 %copy.130 = bf16[2,352,2,2,512]{4,3,2,1,0:T(2,128)(2,1)S(1)} copy(bf16[2,352,2,2,512]{4,2,3,1,0:T(2,128)(2,1)} %bitcast.145) | data formatting | bytes 5767168 | tf_op jit(solution)/shard_map/transpose | solution.py:35
  98.1 3.4 reshape.612
  102.5 2.3 collective-permute-start.2
  104.8 3.8 fusion.34
  111.4 7.2 %all-to-all-start.2 = ((bf16[128,4,2,512]{3,2,1,0:T(2,128)(2,1)}), bf16[128,4,2,512]{3,2,1,0:T(2,128)(2,1)S(1)}, u32[]{:S(2)}, u32[]{:S(2)}) async-start(bf16[128,4,2,512]{3,2,1,0:T(2,128)(2,1)} %bitcast.51), calls=%async_computation.2 | async-start | bytes 2097152 | tf_op jit(solution)/shard_map/all_to_all | solution.py:211
  118.6 6.2 %fusion.10 = f32[2,2,352,32,32]{2,4,3,1,0:T(8,128)S(1)} fusion(bf16[2,2,2048,352]{2,3,1,0:T(8,128)(2,1)} %param.13, s32[]{:T(128)S(6)} %select_n.294, bf16[32,2,32,1024]{3,2,1,0:T(8,128)(2,1)} %copy-done.2), kind=kOutput, calls=%fused_computation.19 | convolution fusion | flops 2952790016 | bytes 12845060 | tf_op jit(solution)/shard_map/secd,egdf->gsecf/dot_general | solution.py:133
  124.9 9.2 %add_bitcast_fusion = f32[2,32,2,32,352]{4,3,1,0,2:T(8,128)} fusion(f32[2,2,352,32,32]{2,4,3,1,0:T(8,128)S(1)} %fusion.10, bf16[32,2,32,1024]{3,2,0,1:T(8,128)(2,1)} %collective-permute-done.17, bf16[2,2,2048,352]{2,3,1,0:T(8,128)(2,1)} %param.13, s32[]{:T(128)S(6)} %select_n.295), kind=kOutput, calls=%fused_computation.12 | convolution fusion | flops 2954231808 | bytes 18612228 | tf_op jit(solution)/shard_map/secd,egdf->gsecf/dot_general | solution.py:135
  134.0 8.2 %convolution_convert_fusion = bf16[2,32,32,2048]{3,2,1,0:T(8,128)(2,1)S(1)} fusion(bf16[2,352,2048,1]{2,1,0,3:T(8,128)(2,1)} %reshape.612, f32[2,32,2,32,352]{4,3,1,0,2:T(8,128)} %add_bitcast_fusion), kind=kOutput, calls=%fused_computation.14 | convolution fusion | flops 2961309696 | bytes 17039360 | tf_op jit(solution)/shard_map/secf,efd->secd/dot_general | solution.py:139
  142.3 3.2 dynamic-slice_bitcast_fusion
  147.8 2.7 collective-permute-start.3
  150.7 6.6 %copy.154 = bf16[8,1,512,512]{3,0,1,2:T(8,128)(2,1)} copy(bf16[8,1,512,512]{3,2,0,1:T(8,128)(2,1)} %bitcast.150) | data formatting | bytes 8388608 | tf_op jit(solution)/shard_map/reshape | solution.py:21
  159.3 9.9 %all-to-all-start.3 = ((bf16[8,1,512,512]{3,0,1,2:T(8,128)(2,1)}), bf16[8,1,512,512]{3,0,1,2:T(8,128)(2,1)}, u32[]{:S(2)}, u32[]{:S(2)}) async-start(bf16[8,1,512,512]{3,0,1,2:T(8,128)(2,1)} %copy.154), calls=%async_computation.3 | async-start | bytes 8388608 | tf_op jit(solution)/shard_map/all_to_all | solution.py:23
  170.5 2.9 collective-permute-start.6
  176.4 65.5 %collective-permute-done.6 = bf16[4,64,3,704]{3,1,2,0:T(8,128)(2,1)S(1)} collective-permute-done((bf16[4,64,3,704]{3,1,2,0:T(8,128)(2,1)S(1)}, bf16[4,64,3,704]{3,1,2,0:T(8,128)(2,1)S(1)}, u32[]{:S(2)}, u32[]{:S(2)}) %collective-permute-start.6) | collective-permute-done | bytes 1081376 | tf_op jit(solution)/shard_map/ppermute | solution.py:55
  241.9 2.5 collective-permute-start.8
  244.7 24.0 %collective-permute-done.8 = bf16[1,4,64,3,704]{4,2,3,1,0:T(8,128)(2,1)} collective-permute-done((bf16[1,4,64,3,704]{4,2,3,1,0:T(8,128)(2,1)S(1)}, bf16[1,4,64,3,704]{4,2,3,1,0:T(8,128)(2,1)}, u32[]{:S(2)}, u32[]{:S(2)}) %collective-permute-start.8) | collective-permute-done | bytes 1081376 | tf_op jit(solution)/shard_map/ppermute | solution.py:63
  268.7 3.5 collective-permute-start.9
  273.2 1.6 gather_fusion
  274.8 21.3 %collective-permute-done.9 = bf16[1,4,64,3,704]{4,2,3,1,0:T(8,128)(2,1)} collective-permute-done((bf16[1,4,64,3,704]{4,2,3,1,0:T(8,128)(2,1)}, bf16[1,4,64,3,704]{4,2,3,1,0:T(8,128)(2,1)}, u32[]{:S(2)}, u32[]{:S(2)}) %collective-permute-start.9) | collective-permute-done | bytes 1081376 | tf_op jit(solution)/shard_map/ppermute | solution.py:63
  296.0 3.4 collective-permute-start.10
  299.5 1.8 maximum_bitcast_fusion
  301.3 8.0 %fusion.5 = bf16[32,2,32,1024]{3,2,0,1:T(8,128)(2,1)} fusion(bf16[32,2,32,1024]{3,2,0,1:T(8,128)(2,1)} %collective-permute-done.18, bf16[2,32,32,2048]{3,2,1,0:T(8,128)(2,1)} %copy-done.5, s32[]{:T(128)S(6)} %select_n.294), kind=kLoop, calls=%fused_computation.11 | loop fusion | flops 8388608 | bytes 12582916 | tf_op jit(solution)/shard_map/convert_element_type | solution.py:143
  309.3 7.8 %reshape.583 = bf16[32,2,32,2,512]{4,3,2,0,1:T(2,128)(2,1)} reshape(bf16[32,2,32,1024]{3,2,0,1:T(8,128)(2,1)} %fusion.5) | data formatting | bytes 8388608 | tf_op jit(solution)/shard_map/reshape | solution.py:143
  317.1 5.2 %copy.131 = bf16[32,2,32,2,512]{4,2,1,0,3:T(8,128)(2,1)} copy(bf16[32,2,32,2,512]{4,3,2,0,1:T(2,128)(2,1)} %reshape.583) | data formatting | bytes 8388608 | tf_op jit(solution)/shard_map/reshape | solution.py:143
  322.3 6.9 %all-to-all-start.1 = ((bf16[64,2,32,512]{3,2,1,0:T(8,128)(2,1)}), bf16[64,2,32,512]{3,2,1,0:T(8,128)(2,1)}, u32[]{:S(2)}, u32[]{:S(2)}) async-start(bf16[64,2,32,512]{3,2,1,0:T(8,128)(2,1)} %bitcast.144), calls=%async_computation.1 | async-start | bytes 8388608 | tf_op jit(solution)/shard_map/all_to_all | solution.py:145
  329.2 1.8 fusion.33
  331.0 1.8 copy.137
  332.8 2.6 convert_element_type.153
  335.4 3.2 maximum_bitcast_fusion.2
  338.7 3.3 maximum_bitcast_fusion.3
  341.9 7.4 %copy.139 = bf16[8,32,4,4,512]{4,3,1,2,0:T(4,128)(2,1)} copy(bf16[8,32,4,4,512]{4,0,2,1,3:T(8,128)(2,1)} %bitcast.58) | data formatting | bytes 8388608 | tf_op jit(solution)/shard_map/transpose | solution.py:25
  349.4 7.7 %reshape_reshape.4 = bf16[2,2,2,32,4,2048]{5,3,4,2,1,0:T(8,128)(2,1)} reshape(bf16[8,32,4,4,512]{4,3,1,2,0:T(4,128)(2,1)} %copy.139) | data formatting | bytes 8388608 | tf_op jit(solution)/shard_map/reshape;reshape | solution.py:28
  357.1 2.0 maximum_bitcast_fusion.1
  360.2 4.3 %pad_maximum_fusion = bf16[4,2,4,64,3,704]{5,3,4,2,1,0:T(8,128)(2,1)} fusion(bf16[1,2,4,64,3,704]{5,3,4,2,1,0:T(8,128)(2,1)S(1)} %copy-done.4, bf16[1,2,4,64,3,704]{5,3,4,2,1,0:T(8,128)(2,1)S(1)} %copy-done.3, bf16[1,2,4,64,3,704]{5,3,4,2,1,0:T(8,128)(2,1)S(1)} %maximum_bitcast_fusion.1, bf16[1,2,4,64,3,704]{5,3,4,2,1,0:T(8,128)(2,1)S(1)} %maximum_bitcast_fusion), kind=kLoop, calls=%fused_computation.7 | loop fusion | flops 12976128 | bytes 17301504 | tf_op jit(solution)/shard_map/stack | solution.py:66
  364.5 8.6 %copy.119 = bf16[4,2,4,64,3,704]{5,3,2,1,0,4:T(8,128)(2,1)} copy(bf16[4,2,4,64,3,704]{5,3,4,2,1,0:T(8,128)(2,1)} %pad_maximum_fusion) | data formatting | bytes 17301504 | tf_op jit(solution)/shard_map/stack | solution.py:66
  373.1 4.8 %convolution_bitcast_fusion = f32[2,256,704]{1,2,0:T(8,128)S(1)} fusion(bf16[32,64,3,704]{3,1,0,2:T(8,128)(2,1)} %bitcast.146, bf16[32,256,64]{1,2,0:T(8,128)(2,1)S(1)} %copy-done.12, pred[32]{0:T(512)(128)(4,1)S(1)} %compare_and_fusion.1), kind=kOutput, calls=%fused_computation.51 | convolution fusion | flops 1476919296 | bytes 11141152 | tf_op jit(solution)/shard_map/tcj,cjgs->gts/dot_general | solution.py:174
  377.9 3.0 fusion.16
  383.9 3.5 collective-permute-start.15
  387.4 2.6 select_select_fusion
  390.0 5.3 %copy.140 = bf16[2,2,2,32,4,2048]{5,4,3,2,1,0:T(4,128)(2,1)} copy(bf16[2,2,2,32,4,2048]{5,3,4,2,1,0:T(8,128)(2,1)S(1)} %select_select_fusion) | data formatting | bytes 8388608
  397.1 3.4 convert_element_type.144
  401.3 3.7 multiply_reduce_fusion
  (130 shorter events, 34.4 us)
Async XLA Ops:
  0.6 271.7 %copy-start = (bf16[2048,64]{0,1:T(8,128)(2,1)S(1)}, bf16[2048,64]{0,1:T(8,128)(2,1)}, u32[]{:S(2)}) copy-start(bf16[2048,64]{0,1:T(8,128)(2,1)} %param.11) | copy-start | bytes 786436
  1.8 2.6 collective-permute-start.13
  4.2 3.8 copy-start.21
  4.4 0.7 copy-start.17
  5.3 13.2 %collective-permute-start.14 = (bf16[256,1024]{0,1:T(8,128)(2,1)S(1)}, bf16[256,1024]{0,1:T(8,128)(2,1)S(1)}, u32[]{:S(2)}, u32[]{:S(2)}) collective-permute-start(bf16[256,1024]{0,1:T(8,128)(2,1)S(1)} %maximum_select_fusion.3), channel_id=1, source_target_pairs={{0,64},{64,0},{1,65},{65,1},{2,66},{66,2},{3,67},{67,3},{4,68},{68... | collective-permute-start | bytes 1572872 | tf_op jit(solution)/shard_map/ppermute | solution.py:39
  18.5 2.1 copy-start.9
  19.3 1.3 copy-start.6
  81.2 3.9 copy-start.2
  81.2 6.2 %copy-start.19 = (bf16[2,64,704]{2,1,0:T(8,128)(2,1)S(1)}, bf16[2,64,704]{2,1,0:T(8,128)(2,1)}, u32[]{:S(2)}) copy-start(bf16[2,64,704]{2,1,0:T(8,128)(2,1)} %param.15) | copy-start | bytes 540676
  81.2 6.2 %copy-start.20 = (bf16[704,64]{0,1:T(8,128)(2,1)S(1)}, bf16[704,64]{0,1:T(8,128)(2,1)}, u32[]{:S(2)}) copy-start(bf16[704,64]{0,1:T(8,128)(2,1)} %param.16) | copy-start | bytes 270340
  81.2 8.7 %copy-start.14 = (bf16[2,352,2048]{2,1,0:T(8,128)(2,1)S(1)}, bf16[2,352,2048]{2,1,0:T(8,128)(2,1)}, u32[]{:S(2)}) copy-start(bf16[2,352,2048]{2,1,0:T(8,128)(2,1)} %param.14) | copy-start | bytes 8650756
  85.1 39.8 %collective-permute-start.17 = (bf16[32,2,32,1024]{3,2,0,1:T(8,128)(2,1)}, bf16[32,2,32,1024]{3,2,0,1:T(8,128)(2,1)}, u32[]{:S(2)}, u32[]{:S(2)}) collective-permute-start(bf16[32,2,32,1024]{3,2,0,1:T(8,128)(2,1)} %copy.128), channel_id=1, source_target_pairs={{0,32},{32,0},{1,33},{33,1},{2,34},{34,2},{3,35},{35,3},{4,36},{36... | collective-permute-start | bytes 12582920 | tf_op jit(solution)/shard_map/ppermute | solution.py:128
  88.2 14.3 %collective-permute-start.1 = (bf16[32,3,704]{2,0,1:T(8,128)(2,1)}, bf16[32,3,704]{2,0,1:T(8,128)(2,1)}, u32[]{:S(2)}, u32[]{:S(2)}) collective-permute-start(bf16[32,3,704]{2,0,1:T(8,128)(2,1)} %get-tuple-element.13), channel_id=1, source_target_pairs={{0,3},{1,0},{2,1},{3,2},{4,7},{5,4},{6,5},{7,6},{8,11},{9,8},{10,9... | collective-permute-start | bytes 405512 | tf_op jit(solution)/shard_map/ppermute | solution.py:63
  89.1 15.6 %collective-permute-start = (bf16[32,3,704]{2,0,1:T(8,128)(2,1)}, bf16[32,3,704]{2,0,1:T(8,128)(2,1)}, u32[]{:S(2)}, u32[]{:S(2)}) collective-permute-start(bf16[32,3,704]{2,0,1:T(8,128)(2,1)} %get-tuple-element.12), channel_id=1, source_target_pairs={{0,1},{1,2},{2,3},{3,0},{4,5},{5,6},{6,7},{7,4},{8,9},{9,10},{10,1... | collective-permute-start | bytes 405512 | tf_op jit(solution)/shard_map/ppermute | solution.py:62
  102.5 45.2 %collective-permute-start.2 = (bf16[32,3,704]{2,0,1:T(8,128)(2,1)}, bf16[32,3,704]{2,0,1:T(8,128)(2,1)S(1)}, u32[]{:S(2)}, u32[]{:S(2)}) collective-permute-start(bf16[32,3,704]{2,0,1:T(8,128)(2,1)} %collective-permute-done.1), channel_id=1, source_target_pairs={{0,3},{1,0},{2,1},{3,2},{4,7},{5,4},{6,5},{7,6},{8,11},{9,8},{10,9... | collective-permute-start | bytes 405512 | tf_op jit(solution)/shard_map/ppermute | solution.py:63
  104.8 52.5 %collective-permute-start.4 = (bf16[32,3,704]{2,0,1:T(8,128)(2,1)}, bf16[32,3,704]{2,0,1:T(8,128)(2,1)S(1)}, u32[]{:S(2)}, u32[]{:S(2)}) collective-permute-start(bf16[32,3,704]{2,0,1:T(8,128)(2,1)} %collective-permute-done), channel_id=1, source_target_pairs={{0,1},{1,2},{2,3},{3,0},{4,5},{5,6},{6,7},{7,4},{8,9},{9,10},{10,1... | collective-permute-start | bytes 405512 | tf_op jit(solution)/shard_map/ppermute | solution.py:62
  111.4 46.9 %all-to-all-start.2 = ((bf16[128,4,2,512]{3,2,1,0:T(2,128)(2,1)}), bf16[128,4,2,512]{3,2,1,0:T(2,128)(2,1)S(1)}, u32[]{:S(2)}, u32[]{:S(2)}) async-start(bf16[128,4,2,512]{3,2,1,0:T(2,128)(2,1)} %bitcast.51), calls=%async_computation.2 | async-start | bytes 2097152 | tf_op jit(solution)/shard_map/all_to_all | solution.py:211
  142.2 4.5 %copy-start.5 = (bf16[2,32,32,2048]{3,2,1,0:T(8,128)(2,1)}, bf16[2,32,32,2048]{3,2,1,0:T(8,128)(2,1)S(1)}, u32[]{:S(2)}) copy-start(bf16[2,32,32,2048]{3,2,1,0:T(8,128)(2,1)S(1)} %convolution_convert_fusion) | copy-start | bytes 25165828
  146.8 154.5 %collective-permute-start.18 = (bf16[32,2,32,1024]{3,2,0,1:T(8,128)(2,1)}, bf16[32,2,32,1024]{3,2,0,1:T(8,128)(2,1)}, u32[]{:S(2)}, u32[]{:S(2)}) collective-permute-start(bf16[32,2,32,1024]{3,2,0,1:T(8,128)(2,1)} %dynamic-slice_bitcast_fusion), channel_id=1, source_target_pairs={{0,32},{32,0},{1,33},{33,1},{2,34},{34,2},{3,35},{35,3},{4,36},{36... | collective-permute-start | bytes 12582920 | tf_op jit(solution)/shard_map/ppermute | solution.py:49
  147.8 9.6 %collective-permute-start.3 = (bf16[32,3,704]{2,0,1:T(8,128)(2,1)S(1)}, bf16[32,3,704]{2,0,1:T(8,128)(2,1)S(1)}, u32[]{:S(2)}, u32[]{:S(2)}) collective-permute-start(bf16[32,3,704]{2,0,1:T(8,128)(2,1)S(1)} %collective-permute-done.2), channel_id=1, source_target_pairs={{0,3},{1,0},{2,1},{3,2},{4,7},{5,4},{6,5},{7,6},{8,11},{9,8},{10,9... | collective-permute-start | bytes 405512 | tf_op jit(solution)/shard_map/ppermute | solution.py:63
  157.3 12.0 %collective-permute-start.5 = (bf16[32,3,704]{2,0,1:T(8,128)(2,1)S(1)}, bf16[32,3,704]{2,0,1:T(8,128)(2,1)S(1)}, u32[]{:S(2)}, u32[]{:S(2)}) collective-permute-start(bf16[32,3,704]{2,0,1:T(8,128)(2,1)S(1)} %collective-permute-done.4), channel_id=1, source_target_pairs={{0,1},{1,2},{2,3},{3,0},{4,5},{5,6},{6,7},{7,4},{8,9},{9,10},{10,1... | collective-permute-start | bytes 405512 | tf_op jit(solution)/shard_map/ppermute | solution.py:62
  158.3 1.0 copy-start.11
  159.3 163.1 %all-to-all-start.3 = ((bf16[8,1,512,512]{3,0,1,2:T(8,128)(2,1)}), bf16[8,1,512,512]{3,0,1,2:T(8,128)(2,1)}, u32[]{:S(2)}, u32[]{:S(2)}) async-start(bf16[8,1,512,512]{3,0,1,2:T(8,128)(2,1)} %copy.154), calls=%async_computation.3 | async-start | bytes 8388608 | tf_op jit(solution)/shard_map/all_to_all | solution.py:23
  169.2 4.3 %copy-start.22 = (s32[2]{0:T(128)S(1)}, s32[2]{0:T(128)}, u32[]{:S(2)}) copy-start(s32[2]{0:T(128)} %param.18) | copy-start | bytes 28
  169.2 103.0 %copy-start.18 = (bf16[256,512]{0,1:T(8,128)(2,1)S(1)}, bf16[256,512]{0,1:T(8,128)(2,1)}, u32[]{:S(2)}) copy-start(bf16[256,512]{0,1:T(8,128)(2,1)} %copy-done.17) | copy-start | bytes 786436
  169.2 103.1 %copy-start.7 = (bf16[256,2048]{0,1:T(8,128)(2,1)S(1)}, bf16[256,2048]{0,1:T(8,128)(2,1)}, u32[]{:S(2)}) copy-start(bf16[256,2048]{0,1:T(8,128)(2,1)} %copy-done.6) | copy-start | bytes 3145732
  170.3 102.4 %copy-start.10 = (bf16[256,1024]{0,1:T(8,128)(2,1)S(1)}, bf16[256,1024]{0,1:T(8,128)(2,1)}, u32[]{:S(2)}) copy-start(bf16[256,1024]{0,1:T(8,128)(2,1)} %copy-done.9) | copy-start | bytes 1572868
  170.5 102.2 %copy-start.8 = (bf16[1,4,64,3,704]{4,2,3,1,0:T(8,128)(2,1)}, bf16[1,4,64,3,704]{4,2,3,1,0:T(8,128)(2,1)S(1)}, u32[]{:S(2)}) copy-start(bf16[1,4,64,3,704]{4,2,3,1,0:T(8,128)(2,1)S(1)} %get-tuple-element.10) | copy-start | bytes 3244036
  170.5 71.3 %collective-permute-start.6 = (bf16[4,64,3,704]{3,1,2,0:T(8,128)(2,1)S(1)}, bf16[4,64,3,704]{3,1,2,0:T(8,128)(2,1)S(1)}, u32[]{:S(2)}, u32[]{:S(2)}) collective-permute-start(bf16[4,64,3,704]{3,1,2,0:T(8,128)(2,1)S(1)} %get-tuple-element.11), channel_id=1, source_target_pairs={{0,4},{4,0},{1,5},{5,1},{2,6},{6,2},{3,7},{7,3},{8,12},{12,8},{9,1... | collective-permute-start | bytes 3244040 | tf_op jit(solution)/shard_map/ppermute | solution.py:55
  175.0 69.5 %collective-permute-start.7 = (bf16[1,4,64,3,704]{4,2,3,1,0:T(8,128)(2,1)S(1)}, bf16[1,4,64,3,704]{4,2,3,1,0:T(8,128)(2,1)S(1)}, u32[]{:S(2)}, u32[]{:S(2)}) collective-permute-start(bf16[1,4,64,3,704]{4,2,3,1,0:T(8,128)(2,1)S(1)} %get-tuple-element.10), channel_id=1, source_target_pairs={{0,8},{8,16},{16,24},{24,0},{1,9},{9,17},{17,25},{25,1},{2,10},{10... | collective-permute-start | bytes 3244040 | tf_op jit(solution)/shard_map/ppermute | solution.py:62
  241.8 30.4 %copy-start.16 = (bf16[4,64,3,704]{3,1,2,0:T(8,128)(2,1)}, bf16[4,64,3,704]{3,1,2,0:T(8,128)(2,1)S(1)}, u32[]{:S(2)}) copy-start(bf16[4,64,3,704]{3,1,2,0:T(8,128)(2,1)S(1)} %collective-permute-done.6) | copy-start | bytes 3244036
  241.9 26.9 %collective-permute-start.8 = (bf16[1,4,64,3,704]{4,2,3,1,0:T(8,128)(2,1)S(1)}, bf16[1,4,64,3,704]{4,2,3,1,0:T(8,128)(2,1)}, u32[]{:S(2)}, u32[]{:S(2)}) collective-permute-start(bf16[1,4,64,3,704]{4,2,3,1,0:T(8,128)(2,1)S(1)} %bitcast.154), channel_id=1, source_target_pairs={{0,24},{8,0},{16,8},{24,16},{1,25},{9,1},{17,9},{25,17},{2,26},{10... | collective-permute-start | bytes 3244040 | tf_op jit(solution)/shard_map/ppermute | solution.py:63
  244.5 30.3 %copy-start.15 = (bf16[1,4,64,3,704]{4,2,3,1,0:T(8,128)(2,1)}, bf16[1,4,64,3,704]{4,2,3,1,0:T(8,128)(2,1)S(1)}, u32[]{:S(2)}) copy-start(bf16[1,4,64,3,704]{4,2,3,1,0:T(8,128)(2,1)S(1)} %collective-permute-done.7) | copy-start | bytes 3244036
  244.5 28.5 %collective-permute-start.11 = (bf16[1,4,64,3,704]{4,2,3,1,0:T(8,128)(2,1)S(1)}, bf16[1,4,64,3,704]{4,2,3,1,0:T(8,128)(2,1)}, u32[]{:S(2)}, u32[]{:S(2)}) collective-permute-start(bf16[1,4,64,3,704]{4,2,3,1,0:T(8,128)(2,1)S(1)} %collective-permute-done.7), channel_id=1, source_target_pairs={{0,8},{8,16},{16,24},{24,0},{1,9},{9,17},{17,25},{25,1},{2,10},{10... | collective-permute-start | bytes 3244040 | tf_op jit(solution)/shard_map/ppermute | solution.py:62
  268.7 27.3 %collective-permute-start.9 = (bf16[1,4,64,3,704]{4,2,3,1,0:T(8,128)(2,1)}, bf16[1,4,64,3,704]{4,2,3,1,0:T(8,128)(2,1)}, u32[]{:S(2)}, u32[]{:S(2)}) collective-permute-start(bf16[1,4,64,3,704]{4,2,3,1,0:T(8,128)(2,1)} %collective-permute-done.8), channel_id=1, source_target_pairs={{0,24},{8,0},{16,8},{24,16},{1,25},{9,1},{17,9},{25,17},{2,26},{10... | collective-permute-start | bytes 3244040 | tf_op jit(solution)/shard_map/ppermute | solution.py:63
  273.1 65.6 %collective-permute-start.12 = (bf16[1,4,64,3,704]{4,2,3,1,0:T(8,128)(2,1)}, bf16[1,4,64,3,704]{4,2,3,1,0:T(8,128)(2,1)}, u32[]{:S(2)}, u32[]{:S(2)}) collective-permute-start(bf16[1,4,64,3,704]{4,2,3,1,0:T(8,128)(2,1)} %collective-permute-done.11), channel_id=1, source_target_pairs={{0,8},{8,16},{16,24},{24,0},{1,9},{9,17},{17,25},{25,1},{2,10},{10... | collective-permute-start | bytes 3244040 | tf_op jit(solution)/shard_map/ppermute | solution.py:62
  296.0 61.1 %collective-permute-start.10 = (bf16[1,4,64,3,704]{4,2,3,1,0:T(8,128)(2,1)}, bf16[1,4,64,3,704]{4,2,3,1,0:T(8,128)(2,1)}, u32[]{:S(2)}, u32[]{:S(2)}) collective-permute-start(bf16[1,4,64,3,704]{4,2,3,1,0:T(8,128)(2,1)} %collective-permute-done.9), channel_id=1, source_target_pairs={{0,24},{8,0},{16,8},{24,16},{1,25},{9,1},{17,9},{25,17},{2,26},{10... | collective-permute-start | bytes 3244040 | tf_op jit(solution)/shard_map/ppermute | solution.py:63
  322.3 74.8 %all-to-all-start.1 = ((bf16[64,2,32,512]{3,2,1,0:T(8,128)(2,1)}), bf16[64,2,32,512]{3,2,1,0:T(8,128)(2,1)}, u32[]{:S(2)}, u32[]{:S(2)}) async-start(bf16[64,2,32,512]{3,2,1,0:T(8,128)(2,1)} %bitcast.144), calls=%async_computation.1 | async-start | bytes 8388608 | tf_op jit(solution)/shard_map/all_to_all | solution.py:145
  357.1 2.4 copy-start.3
  357.1 3.1 copy-start.4
  364.4 8.6 %copy-start.12 = (bf16[32,256,64]{1,2,0:T(8,128)(2,1)S(1)}, bf16[32,256,64]{1,2,0:T(8,128)(2,1)}, u32[]{:S(2)}) copy-start(bf16[32,256,64]{1,2,0:T(8,128)(2,1)} %gather_fusion) | copy-start | bytes 3145732
  383.0 4.4 %copy-start.13 = (bf16[2,32,4,2048]{3,1,2,0:T(8,128)(2,1)S(1)}, bf16[2,32,4,2048]{3,1,2,0:T(8,128)(2,1)}, u32[]{:S(2)}) copy-start(bf16[2,32,4,2048]{3,1,2,0:T(8,128)(2,1)} %convert_element_type.153) | copy-start | bytes 3145732
  383.9 11.4 %collective-permute-start.15 = (bf16[256,1024]{1,0:T(8,128)(2,1)S(1)}, bf16[256,1024]{1,0:T(8,128)(2,1)S(1)}, u32[]{:S(2)}, u32[]{:S(2)}) collective-permute-start(bf16[256,1024]{1,0:T(8,128)(2,1)S(1)} %constant_dynamic-slice_fusion.1), channel_id=1, source_target_pairs={{0,32},{32,0},{1,33},{33,1},{2,34},{34,2},{3,35},{35,3},{4,36},{36... | collective-permute-start | bytes 1572872 | tf_op jit(solution)/shard_map/ppermute | solution.py:49
  395.5 9.5 %collective-permute-start.16 = (bf16[256,512]{1,0:T(8,128)(2,1)S(1)}, bf16[256,512]{1,0:T(8,128)(2,1)S(1)}, u32[]{:S(2)}, u32[]{:S(2)}) collective-permute-start(bf16[256,512]{1,0:T(8,128)(2,1)S(1)} %constant_dynamic-slice_fusion), channel_id=1, source_target_pairs={{0,64},{64,0},{1,65},{65,1},{2,66},{66,2},{3,67},{67,3},{4,68},{68... | collective-permute-start | bytes 786440 | tf_op jit(solution)/shard_map/ppermute | solution.py:49
  401.3 4.6 %copy-start.1 = (bf16[2048,64]{0,1:T(8,128)(2,1)S(1)}, bf16[2048,64]{0,1:T(8,128)(2,1)}, u32[]{:S(2)}) copy-start(bf16[2048,64]{0,1:T(8,128)(2,1)} %param.11) | copy-start | bytes 786436
